TPU v7x, 128 devices: a whole 4x4x4 slice. The times are simulated.
128 devices in a mesh: ctx: 8 (over z, x_hi), head: 16 (over x_lo, y, core).
Axes of the slice: x: 4 (x_hi: 2, x_lo: 2; x = x_hi * 2 + x_lo), y: 4, z: 4, core: 2. Of those that a mesh axis runs over, the one named last changes fastest.
Arguments:
- queries: bfloat16 [32768, 4096], P(('ctx', 'head')), may hold values from -8 to 8
- keys: bfloat16 [32768, 2048], P(('ctx', 'head')), may hold values from -8 to 8
- values: bfloat16 [32768, 2048], P(('ctx', 'head')), may hold values from -18 to 18
- grad_out: bfloat16 [32768, 4096], P(('ctx', 'head')), may hold values from -18 to 18
Outputs:
- attended: bfloat16 [32768, 4096], P(('ctx', 'head'))
- grad_queries: bfloat16 [32768, 4096], P(('ctx', 'head'))
- grad_keys: bfloat16 [32768, 2048], P(('ctx', 'head'))
- grad_values: bfloat16 [32768, 2048], P(('ctx', 'head'))
All inputs are finite; a program needn't handle non-finite values.
Results may differ from a plain program's by a relative error of at most 0.02.
Values may be sent and summed in bfloat16 or wider, within the bound.
No kernel may reach another device: no remote copies, remote signals or barrier semaphores. Data moves between devices by JAX's collectives and lax.ppermute only.
A program may use at most 256 MiB of HBM per device.

v0:
```python
import jax
import jax.numpy as jnp
from jax import lax
from jax.sharding import PartitionSpec as P

HD = 128
QH = 32
KVH = 16
WIN = 1024
QPRE = 168
BLK = 256


def shifted(block, axis, distance):
    devices = range(lax.axis_size(axis))
    route = [(i - distance, i) for i in devices if i - distance in devices]
    return lax.ppermute(block, axis, route)


def place_blocks(stacked, reach):
    block_total = stacked.shape[0]
    shared_heads = stacked.shape[1]
    block_rows = stacked.shape[3]
    head_width = stacked.shape[4]
    total = None
    for offset in range(reach + 1):
        piece = stacked[:, :, offset]
        padded = jnp.pad(piece, ((offset, reach - offset), (0, 0), (0, 0), (0, 0)))
        total = padded if total is None else total + padded
    total = jnp.transpose(total, (0, 2, 1, 3))
    return total.reshape((block_total + reach) * block_rows, shared_heads, head_width)


def attend(queries, keys_ext, values_ext, grads, first_query):
    query_count = queries.shape[0]
    query_heads = queries.shape[1]
    shared_heads = keys_ext.shape[1]
    head_width = queries.shape[2]
    group_size = query_heads // shared_heads
    block_rows = min(BLK, query_count)
    reach = WIN // block_rows
    key_span = WIN + block_rows
    block_total = query_count // block_rows
    scale = QPRE ** (-0.5)
    query_major = jnp.transpose(
        queries.reshape(query_count, shared_heads, group_size, head_width), (1, 2, 0, 3)
    )
    grad_major = jnp.transpose(
        grads.reshape(query_count, shared_heads, group_size, head_width), (1, 2, 0, 3)
    )
    key_major = jnp.transpose(keys_ext, (1, 0, 2))
    value_major = jnp.transpose(values_ext, (1, 0, 2))

    def block_step(carry, block):
        first_row = block * block_rows
        query_stack = lax.dynamic_slice_in_dim(query_major, first_row, block_rows, 2)
        grad_stack = lax.dynamic_slice_in_dim(grad_major, first_row, block_rows, 2)
        key_stack = lax.dynamic_slice_in_dim(key_major, first_row, key_span, 1)
        value_stack = lax.dynamic_slice_in_dim(value_major, first_row, key_span, 1)
        query_pos = first_query + first_row + jnp.arange(block_rows, dtype=jnp.int32)
        key_pos = first_query - WIN + first_row + jnp.arange(key_span, dtype=jnp.int32)
        distance = query_pos[:, None] - key_pos[None, :]
        allowed = (distance >= 0) & (distance < WIN) & (key_pos[None, :] >= 0)
        scores = (
            jnp.einsum("sgqd,skd->sgqk", query_stack, key_stack, preferred_element_type=jnp.float32)
            * scale
        )
        scores = jnp.where(allowed[None, None], scores, -jnp.inf)
        largest = jnp.max(scores, axis=-1, keepdims=True)
        unnormed = jnp.exp(scores - largest)
        probs = unnormed / jnp.sum(unnormed, axis=-1, keepdims=True)
        probs_low = probs.astype(jnp.bfloat16)
        output_stack = jnp.einsum(
            "sgqk,skd->sgqd", probs_low, value_stack, preferred_element_type=jnp.float32
        ).astype(jnp.bfloat16)
        grad_probs = jnp.einsum(
            "sgqd,skd->sgqk", grad_stack, value_stack, preferred_element_type=jnp.float32
        )
        inner = jnp.sum(
            grad_stack.astype(jnp.float32) * output_stack.astype(jnp.float32),
            axis=-1,
            keepdims=True,
        )
        grad_scores = (probs * (grad_probs - inner) * scale).astype(jnp.bfloat16)
        grad_query = jnp.einsum(
            "sgqk,skd->sgqd", grad_scores, key_stack, preferred_element_type=jnp.float32
        ).astype(jnp.bfloat16)
        grad_key = jnp.einsum(
            "sgqk,sgqd->skd", grad_scores, query_stack, preferred_element_type=jnp.float32
        )
        grad_value = jnp.einsum(
            "sgqk,sgqd->skd", probs_low, grad_stack, preferred_element_type=jnp.float32
        )
        return (carry, (output_stack, grad_query, grad_key, grad_value))

    unused, (outputs, grad_queries, key_terms, value_terms) = lax.scan(
        block_step, None, jnp.arange(block_total, dtype=jnp.int32)
    )
    attended = jnp.transpose(outputs, (0, 3, 1, 2, 4)).reshape(query_count, query_heads, head_width)
    grad_queries = jnp.transpose(grad_queries, (0, 3, 1, 2, 4)).reshape(
        query_count, query_heads, head_width
    )
    key_terms = key_terms.reshape(block_total, shared_heads, reach + 1, block_rows, head_width)
    value_terms = value_terms.reshape(block_total, shared_heads, reach + 1, block_rows, head_width)
    key_total = place_blocks(key_terms, reach)
    value_total = place_blocks(value_terms, reach)
    return (attended, grad_queries, key_total, value_total)


def body(queries, keys, values, grad_out):
    token_count = queries.shape[0]
    query_rows = queries.reshape(token_count, QH, HD)
    key_rows = keys.reshape(token_count, KVH, HD)
    value_rows = values.reshape(token_count, KVH, HD)
    grad_rows = grad_out.reshape(token_count, QH, HD)
    group_queries, group_keys, group_values, group_grads = (
        lax.all_to_all(query_rows, "head", split_axis=1, concat_axis=0, tiled=True),
        lax.all_to_all(key_rows, "head", split_axis=1, concat_axis=0, tiled=True),
        lax.all_to_all(value_rows, "head", split_axis=1, concat_axis=0, tiled=True),
        lax.all_to_all(grad_rows, "head", split_axis=1, concat_axis=0, tiled=True),
    )
    group_rows = group_queries.shape[0]
    first_query = lax.axis_index("ctx") * group_rows
    key_tail, value_tail = shifted(
        (group_keys[group_rows - WIN :], group_values[group_rows - WIN :]), "ctx", 1
    )
    keys_ext = jnp.concatenate([key_tail, group_keys], axis=0)
    values_ext = jnp.concatenate([value_tail, group_values], axis=0)
    attended_group, grad_query_group, key_total, value_total = attend(
        group_queries, keys_ext, values_ext, group_grads, first_query
    )
    key_back, value_back = (
        shifted(key_total[:WIN].astype(jnp.bfloat16), "ctx", -1).astype(jnp.float32),
        shifted(value_total[:WIN].astype(jnp.bfloat16), "ctx", -1).astype(jnp.float32),
    )
    key_grad = jnp.concatenate(
        [key_total[WIN:group_rows], key_total[group_rows:] + key_back], axis=0
    ).astype(jnp.bfloat16)
    value_grad = jnp.concatenate(
        [value_total[WIN:group_rows], value_total[group_rows:] + value_back], axis=0
    ).astype(jnp.bfloat16)
    attended, grad_queries, key_out, value_out = (
        lax.all_to_all(attended_group, "head", split_axis=0, concat_axis=1, tiled=True),
        lax.all_to_all(grad_query_group, "head", split_axis=0, concat_axis=1, tiled=True),
        lax.all_to_all(key_grad, "head", split_axis=0, concat_axis=1, tiled=True),
        lax.all_to_all(value_grad, "head", split_axis=0, concat_axis=1, tiled=True),
    )
    return (
        attended.reshape(token_count, QH * HD),
        grad_queries.reshape(token_count, QH * HD),
        key_out.reshape(token_count, KVH * HD),
        value_out.reshape(token_count, KVH * HD),
    )


def solution(mesh):
    placed = (
        P(("ctx", "head"), None),
        P(("ctx", "head"), None),
        P(("ctx", "head"), None),
        P(("ctx", "head"), None),
    )
    return jax.shard_map(
        body,
        mesh=mesh,
        in_specs=placed,
        out_specs=(
            P(("ctx", "head"), None),
            P(("ctx", "head"), None),
            P(("ctx", "head"), None),
            P(("ctx", "head"), None),
        ),
        check_vma=False,
    )
```

profile of v0, /device:TPU:121, one launch (start us, length us, event | category | flops | bytes accessed | tf_op | source)
XLA Modules:
  0.0 591.2 jit_solution(15837068695838844682)
XLA Ops:
  3.0 5.9 %all-to-all-start.2 = ((bf16[256,16,128]{0,2,1:T(8,128)(2,1)}), bf16[256,16,128]{0,2,1:T(8,128)(2,1)S(1)}, u32[]{:S(2)}, u32[]{:S(2)}) async-start(bf16[256,16,128]{0,2,1:T(8,128)(2,1)} %bitcast.27), calls=%async_computation.2 | async-start | bytes 2097152 | tf_op jit(solution)/shard_map/all_to_all | solution.py:119
  10.2 13.7 %all-to-all-done.2 = bf16[256,16,128]{0,2,1:T(8,128)(2,1)S(1)} async-done(((bf16[256,16,128]{0,2,1:T(8,128)(2,1)}), bf16[256,16,128]{0,2,1:T(8,128)(2,1)S(1)}, u32[]{:S(2)}, u32[]{:S(2)}) %all-to-all-start.2) | async-done | bytes 1048608 | tf_op jit(solution)/shard_map/all_to_all | solution.py:119
  23.9 5.2 all-to-all-start.1
  29.0 4.1 copy.149
  33.1 10.9 %all-to-all-done.1 = bf16[256,16,128]{2,0,1:T(8,128)(2,1)S(1)} async-done(((bf16[256,16,128]{2,0,1:T(8,128)(2,1)}), bf16[256,16,128]{2,0,1:T(8,128)(2,1)S(1)}, u32[]{:S(2)}, u32[]{:S(2)}) %all-to-all-start.1) | async-done | bytes 1048608 | tf_op jit(solution)/shard_map/all_to_all | solution.py:118
  44.0 5.3 all-to-all-start
  49.3 4.1 copy.155
  53.4 25.1 %all-to-all-done = bf16[256,32,128]{0,2,1:T(8,128)(2,1)S(1)} async-done(((bf16[256,32,128]{0,2,1:T(8,128)(2,1)}), bf16[256,32,128]{0,2,1:T(8,128)(2,1)S(1)}, u32[]{:S(2)}, u32[]{:S(2)}) %all-to-all-start) | async-done | bytes 2097184 | tf_op jit(solution)/shard_map/all_to_all | solution.py:117
  78.5 4.5 all-to-all-start.3
  86.9 4.3 collective-permute-start.1
  93.3 21.5 %collective-permute-done.1 = bf16[1024,1,128]{2,0,1:T(8,128)(2,1)S(1)} collective-permute-done((bf16[1024,1,128]{2,0,1:T(8,128)(2,1)}, bf16[1024,1,128]{2,0,1:T(8,128)(2,1)S(1)}, u32[]{:S(2)}, u32[]{:S(2)}) %collective-permute-start.1) | collective-permute-done | bytes 262176 | tf_op jit(solution)/shard_map/ppermute | solution.py:17
  124.0 3.9 copy.157
  128.0 303.8 %while.18 = (s32[]{:T(128)}, bf16[16,1,2,256,128]{4,3,0,2,1:T(8,128)(2,1)}, bf16[16,1,2,256,128]{4,3,0,2,1:T(8,128)(2,1)}, f32[16,1,1280,128]{3,2,1,0:T(8,128)},...) while((s32[]{:T(128)}, ...), condition=%wide.region_4.5_spmd, body=%wide.region_0.4_spmd.sunk | while | flops 1015878400 | bytes 20998960 | solution.py:96
  319.5 3.6 fusion.94
  338.5 3.6 fusion.94
  376.5 3.6 fusion.94
  395.5 3.6 fusion.94
  431.8 8.4 %slice_bitcast_fusion.4 = (f32[16,1,256,128]{3,2,0,1:T(8,128)S(1)}, f32[16,1,256,128]{3,2,0,1:T(8,128)}, f32[16,1,256,128]{3,2,0,1:T(8,128)}, f32[16,1,256,128]{3,2,0,1:T(8,128)}, f32[16,1,256,128]{3,2,0,1:T(8,128)}) fusion(f32[16,1,5,256,128]{4,3,2,0,1:T(8,128)} %bitcast.216), kind=kLoop, calls=%fused_computation.61 | loop fusion | bytes 20971520 | tf_op jit(solution)/shard_map/squeeze | solution.py:27
  440.2 6.1 %fusion.51 = (bf16[20,1,256,128]{3,2,0,1:T(8,128)(2,1)S(1)}, f32[20,1,256,128]{3,2,0,1:T(8,128)}) fusion(f32[16,1,256,128]{3,2,0,1:T(8,128)} %get-tuple-element.266, f32[16,1,256,128]{3,2,0,1:T(8,128)} %get-tuple-element.267, f32[16,1,256,128]{3,2,0,1:T(8,128)} %get-tuple-element.264, f32[16,1,256,128]{3,2,0,1:T(8,128)} %get-tuple-element.265, ...), kind=kLoop, calls=%fused_computation.76 | loop fusion | flops 3276800 | bytes 14417920 | tf_op jit(solution)/shard_map/convert.4
  454.7 5.2 fusion.52
  461.8 4.1 collective-permute-start.2
  469.2 7.8 %all-to-all-start.7 = ((bf16[16,2,16384]{2,1,0:T(2,128)(2,1)}), bf16[16,2,16384]{2,1,0:T(2,128)(2,1)S(1)}, u32[]{:S(2)}, u32[]{:S(2)}) async-start(bf16[16,2,16384]{2,1,0:T(2,128)(2,1)} %reshape.320), calls=%async_computation.7 | async-start | bytes 2097152 | tf_op jit(solution)/shard_map/all_to_all | solution.py:146
  481.8 10.0 %all-to-all-done.7 = bf16[16,2,16384]{2,1,0:T(2,128)(2,1)S(1)} async-done(((bf16[16,2,16384]{2,1,0:T(2,128)(2,1)}), bf16[16,2,16384]{2,1,0:T(2,128)(2,1)S(1)}, u32[]{:S(2)}, u32[]{:S(2)}) %all-to-all-start.7) | async-done | bytes 1048608 | tf_op jit(solution)/shard_map/all_to_all | solution.py:146
  491.9 5.2 all-to-all-start.6
  497.1 5.8 copy.162
  502.9 9.2 %all-to-all-done.6 = bf16[16,2,16384]{2,1,0:T(2,128)(2,1)S(1)} async-done(((bf16[16,2,16384]{2,1,0:T(2,128)(2,1)}), bf16[16,2,16384]{2,1,0:T(2,128)(2,1)S(1)}, u32[]{:S(2)}, u32[]{:S(2)}) %all-to-all-start.6) | async-done | bytes 1048608 | tf_op jit(solution)/shard_map/all_to_all | solution.py:145
  513.0 5.3 all-to-all-start.4
  518.3 5.8 copy.166
  524.1 23.5 %all-to-all-done.4 = bf16[4096,2,128]{2,1,0:T(2,128)(2,1)S(1)} async-done(((bf16[4096,2,128]{2,1,0:T(2,128)(2,1)}), bf16[4096,2,128]{2,1,0:T(2,128)(2,1)S(1)}, u32[]{:S(2)}, u32[]{:S(2)}) %all-to-all-start.4) | async-done | bytes 2097184 | tf_op jit(solution)/shard_map/all_to_all | solution.py:143
  548.8 4.5 all-to-all-start.5
  570.6 12.0 %all-to-all-done.5 = bf16[4096,2,128]{2,1,0:T(2,128)(2,1)} async-done(((bf16[4096,2,128]{2,1,0:T(2,128)(2,1)}), bf16[4096,2,128]{2,1,0:T(2,128)(2,1)}, u32[]{:S(2)}, u32[]{:S(2)}) %all-to-all-start.5) | async-done | bytes 2097184 | tf_op jit(solution)/shard_map/all_to_all | solution.py:144
  587.1 4.2 copy.182
  (329 shorter events, 338.7 us)
Async XLA Ops:
  0.6 8.3 %copy-start = (bf16[256,2048]{1,0:T(8,128)(2,1)S(1)}, bf16[256,2048]{1,0:T(8,128)(2,1)}, u32[]{:S(2)}) copy-start(bf16[256,2048]{1,0:T(8,128)(2,1)} %param.7) | copy-start | bytes 3145732
  3.0 20.9 %all-to-all-start.2 = ((bf16[256,16,128]{0,2,1:T(8,128)(2,1)}), bf16[256,16,128]{0,2,1:T(8,128)(2,1)S(1)}, u32[]{:S(2)}, u32[]{:S(2)}) async-start(bf16[256,16,128]{0,2,1:T(8,128)(2,1)} %bitcast.27), calls=%async_computation.2 | async-start | bytes 2097152 | tf_op jit(solution)/shard_map/all_to_all | solution.py:119
  23.9 9.2 %copy-start.10 = (bf16[256,16,128]{0,2,1:T(8,128)(2,1)}, bf16[256,16,128]{0,2,1:T(8,128)(2,1)S(1)}, u32[]{:S(2)}) copy-start(bf16[256,16,128]{0,2,1:T(8,128)(2,1)S(1)} %all-to-all-done.2) | copy-start | bytes 3145732
  23.9 20.1 %all-to-all-start.1 = ((bf16[256,16,128]{2,0,1:T(8,128)(2,1)}), bf16[256,16,128]{2,0,1:T(8,128)(2,1)S(1)}, u32[]{:S(2)}, u32[]{:S(2)}) async-start(bf16[256,16,128]{2,0,1:T(8,128)(2,1)} %copy_bitcast_fusion), calls=%async_computation.1 | async-start | bytes 2097152 | tf_op jit(solution)/shard_map/all_to_all | solution.py:118
  44.0 34.5 %all-to-all-start = ((bf16[256,32,128]{0,2,1:T(8,128)(2,1)}), bf16[256,32,128]{0,2,1:T(8,128)(2,1)S(1)}, u32[]{:S(2)}, u32[]{:S(2)}) async-start(bf16[256,32,128]{0,2,1:T(8,128)(2,1)} %bitcast.219), calls=%async_computation | async-start | bytes 4194304 | tf_op jit(solution)/shard_map/all_to_all | solution.py:117
  78.5 45.5 %all-to-all-start.3 = ((bf16[256,32,128]{0,2,1:T(8,128)(2,1)}), bf16[256,32,128]{0,2,1:T(8,128)(2,1)}, u32[]{:S(2)}, u32[]{:S(2)}) async-start(bf16[256,32,128]{0,2,1:T(8,128)(2,1)} %bitcast.218), calls=%async_computation.3 | async-start | bytes 4194304 | tf_op jit(solution)/shard_map/all_to_all | solution.py:120
  86.9 27.9 %collective-permute-start.1 = (bf16[1024,1,128]{2,0,1:T(8,128)(2,1)}, bf16[1024,1,128]{2,0,1:T(8,128)(2,1)S(1)}, u32[]{:S(2)}, u32[]{:S(2)}) collective-permute-start(bf16[1024,1,128]{2,0,1:T(8,128)(2,1)} %bitcast.30), channel_id=1, source_target_pairs={{0,16},{16,32},{32,48},{48,64},{64,80},{80,96},{96,112},{1,17},{17... | collective-permute-start | bytes 786440 | tf_op jit(solution)/shard_map/ppermute | solution.py:17
  91.3 29.1 %collective-permute-start = (bf16[1024,1,128]{2,0,1:T(8,128)(2,1)S(1)}, bf16[1024,1,128]{2,0,1:T(8,128)(2,1)S(1)}, u32[]{:S(2)}, u32[]{:S(2)}) collective-permute-start(bf16[1024,1,128]{2,0,1:T(8,128)(2,1)S(1)} %bitcast.239), channel_id=1, source_target_pairs={{0,16},{16,32},{32,48},{48,64},{64,80},{80,96},{96,112},{1,17},{17... | collective-permute-start | bytes 786440 | tf_op jit(solution)/shard_map/ppermute | solution.py:17
  431.8 17.0 %slice-start = ((s8[10485760]{0:T(1024)(128)(4,1)}), s8[4194304]{0:T(1024)(128)(4,1)S(1)}, s32[]{:S(2)}) async-start(s8[10485760]{0:T(1024)(128)(4,1)} %bitcast.213), calls=%async_computation.8 | async-start | bytes 8388608
  431.8 17.0 %slice-start.1 = ((s8[10485760]{0:T(1024)(128)(4,1)}), s8[4194304]{0:T(1024)(128)(4,1)S(1)}, s32[]{:S(2)}) async-start(s8[10485760]{0:T(1024)(128)(4,1)} %bitcast.213), calls=%async_computation.9 | async-start | bytes 8388608
  440.2 8.6 %slice-start.2 = ((s8[10485760]{0:T(1024)(128)(4,1)}), s8[2097152]{0:T(1024)(128)(4,1)S(1)}, s32[]{:S(2)}) async-start(s8[10485760]{0:T(1024)(128)(4,1)} %bitcast.213), calls=%async_computation.10 | async-start | bytes 4194304
  446.3 2.5 copy-start.7
  446.3 19.5 %collective-permute-start.3 = (bf16[1024,1,128]{2,0,1:T(8,128)(2,1)S(1)}, bf16[1024,1,128]{2,0,1:T(8,128)(2,1)S(1)}, u32[]{:S(2)}, u32[]{:S(2)}) collective-permute-start(bf16[1024,1,128]{2,0,1:T(8,128)(2,1)S(1)} %bitcast.238), channel_id=1, source_target_pairs={{16,0},{32,16},{48,32},{64,48},{80,64},{96,80},{112,96},{17,1},{33... | collective-permute-start | bytes 786440 | tf_op jit(solution)/shard_map/ppermute | solution.py:17
  452.3 2.4 copy-start.2
  460.0 1.1 copy-start.5
  461.8 16.3 %collective-permute-start.2 = (bf16[1024,1,128]{2,0,1:T(8,128)(2,1)}, bf16[1024,1,128]{2,0,1:T(8,128)(2,1)}, u32[]{:S(2)}, u32[]{:S(2)}) collective-permute-start(bf16[1024,1,128]{2,0,1:T(8,128)(2,1)} %bitcast.58), channel_id=1, source_target_pairs={{16,0},{32,16},{48,32},{64,48},{80,64},{96,80},{112,96},{17,1},{33... | collective-permute-start | bytes 786440 | tf_op jit(solution)/shard_map/ppermute | solution.py:17
  468.1 8.9 %copy-start.6 = (bf16[20,1,256,128]{3,2,0,1:T(8,128)(2,1)S(1)}, bf16[20,1,256,128]{3,2,0,1:T(8,128)(2,1)}, u32[]{:S(2)}) copy-start(bf16[20,1,256,128]{3,2,0,1:T(8,128)(2,1)} %copy-done.5) | copy-start | bytes 3932164
  469.2 22.7 %all-to-all-start.7 = ((bf16[16,2,16384]{2,1,0:T(2,128)(2,1)}), bf16[16,2,16384]{2,1,0:T(2,128)(2,1)S(1)}, u32[]{:S(2)}, u32[]{:S(2)}) async-start(bf16[16,2,16384]{2,1,0:T(2,128)(2,1)} %reshape.320), calls=%async_computation.7 | async-start | bytes 2097152 | tf_op jit(solution)/shard_map/all_to_all | solution.py:146
  491.9 20.2 %all-to-all-start.6 = ((bf16[16,2,16384]{2,1,0:T(2,128)(2,1)}), bf16[16,2,16384]{2,1,0:T(2,128)(2,1)S(1)}, u32[]{:S(2)}, u32[]{:S(2)}) async-start(bf16[16,2,16384]{2,1,0:T(2,128)(2,1)} %reshape.318), calls=%async_computation.6 | async-start | bytes 2097152 | tf_op jit(solution)/shard_map/all_to_all | solution.py:145
  512.1 1.0 copy-start.8
  513.0 34.5 %all-to-all-start.4 = ((bf16[4096,2,128]{2,1,0:T(2,128)(2,1)}), bf16[4096,2,128]{2,1,0:T(2,128)(2,1)S(1)}, u32[]{:S(2)}, u32[]{:S(2)}) async-start(bf16[4096,2,128]{2,1,0:T(2,128)(2,1)} %copy.162), calls=%async_computation.4 | async-start | bytes 4194304 | tf_op jit(solution)/shard_map/all_to_all | solution.py:143
  547.5 1.3 copy-start.3
  548.8 33.8 %all-to-all-start.5 = ((bf16[4096,2,128]{2,1,0:T(2,128)(2,1)}), bf16[4096,2,128]{2,1,0:T(2,128)(2,1)}, u32[]{:S(2)}, u32[]{:S(2)}) async-start(bf16[4096,2,128]{2,1,0:T(2,128)(2,1)} %copy.166), calls=%async_computation.5 | async-start | bytes 4194304 | tf_op jit(solution)/shard_map/all_to_all | solution.py:144
  555.5 3.0 copy-start.9
  559.7 3.6 copy-start.4
  587.1 4.2 copy-start.1
where the time goes:
time: 596 us; the launch traced here: 591 us
  matrix products  214 us (36%)
  waiting for transfers between devices  129 us (22%)
  local copies, waits for them, and re-layouts  120 us (20%)
  other arithmetic  58.2 us (10%)
  starting transfers between devices  56.3 us (9%)
  loops' own time  11.8 us (2%)
    sub x16, matrix products, block_step(): unnormed = jnp.exp(scores - largest)  57.1 us
    dot_general x16, matrix products, block_step(): jnp.einsum('sgqd,skd->sgqk', grad_stack, value_stack, preferred_element_t...  38.9 us
    dot_general x16, matrix products, block_step(): jnp.einsum('sgqk,sgqd->skd', grad_scores, query_stack, preferred_element_...  37 us
    dot_general x16, matrix products, block_step(): jnp.einsum('sgqk,skd->sgqd', grad_scores, key_stack, preferred_element_ty...  34.2 us
    convert_element_type x16, other arithmetic, block_step(): probs_low = probs.astype(jnp.bfloat16)  32.3 us
    unnamed x41, local copies, waits for them, and re-layouts  30.2 us
    all_to_all x1, waiting for transfers between devices, body(): lax.all_to_all(query_rows, 'head', split_axis=1, concat_axis=0, tiled=True)  25.1 us
    dot_general x16, matrix products, block_step(): jnp.einsum('sgqk,skd->sgqd', probs_low, value_stack, preferred_element_ty...  25 us
  transfers between devices with their start and end apart: 12, of which 9 were waited for; matrix products, arithmetic and copies ran while one was open for 12% of the time, Pallas kernels for 0%

commit v1 on v0

v1 whole, which is shorter than its diff:
```python
import functools

import jax
import jax.numpy as jnp
from jax import lax
from jax.experimental import pallas as pl
from jax.experimental.pallas import tpu as pltpu
from jax.sharding import PartitionSpec as P

HD = 128
QH = 32
KVH = 16
WIN = 1024
QPRE = 168
BLK = 256


def shifted(block, axis, distance):
    devices = range(lax.axis_size(axis))
    route = [(i - distance, i) for i in devices if i - distance in devices]
    return lax.ppermute(block, axis, route)


def attend_kernel(first_ref, q_ref, g_ref, k_ref, v_ref, o_ref, dq_ref, dk_ref, dv_ref):
    block = pl.program_id(0)
    rows = q_ref.shape[0]
    group = q_ref.shape[1] // HD
    span = WIN + rows
    scale = QPRE ** (-0.5)

    @pl.when(block == 0)
    def _():
        dk_ref[...] = jnp.zeros_like(dk_ref)
        dv_ref[...] = jnp.zeros_like(dv_ref)

    start = pl.multiple_of(block * rows, rows)
    k_win = k_ref[pl.ds(start, span), :]
    v_win = v_ref[pl.ds(start, span), :]
    row_id = lax.broadcasted_iota(jnp.int32, (rows, span), 0)
    col_id = lax.broadcasted_iota(jnp.int32, (rows, span), 1)
    distance = row_id + WIN - col_id
    key_pos = first_ref[0] - WIN + start + col_id
    allowed = (distance >= 0) & (distance < WIN) & (key_pos >= 0)
    dk_acc = jnp.zeros((span, HD), jnp.float32)
    dv_acc = jnp.zeros((span, HD), jnp.float32)
    nt = (((1,), (1,)), ((), ()))
    tn = (((0,), (0,)), ((), ()))
    for h in range(group):
        q = q_ref[:, h * HD:(h + 1) * HD]
        g = g_ref[:, h * HD:(h + 1) * HD]
        scores = lax.dot_general(q, k_win, nt, preferred_element_type=jnp.float32) * scale
        scores = jnp.where(allowed, scores, -jnp.inf)
        largest = jnp.max(scores, axis=-1, keepdims=True)
        unnormed = jnp.exp(scores - largest)
        probs = unnormed / jnp.sum(unnormed, axis=-1, keepdims=True)
        probs_low = probs.astype(jnp.bfloat16)
        out = jnp.dot(probs_low, v_win, preferred_element_type=jnp.float32).astype(jnp.bfloat16)
        o_ref[:, h * HD:(h + 1) * HD] = out
        grad_probs = lax.dot_general(g, v_win, nt, preferred_element_type=jnp.float32)
        inner = jnp.sum(g.astype(jnp.float32) * out.astype(jnp.float32), axis=-1, keepdims=True)
        grad_scores = (probs * (grad_probs - inner) * scale).astype(jnp.bfloat16)
        dq_ref[:, h * HD:(h + 1) * HD] = jnp.dot(
            grad_scores, k_win, preferred_element_type=jnp.float32
        ).astype(jnp.bfloat16)
        dk_acc = dk_acc + lax.dot_general(grad_scores, q, tn, preferred_element_type=jnp.float32)
        dv_acc = dv_acc + lax.dot_general(probs_low, g, tn, preferred_element_type=jnp.float32)
    dk_ref[pl.ds(start, span), :] += dk_acc
    dv_ref[pl.ds(start, span), :] += dv_acc


def attend(queries, keys_ext, values_ext, grads, first_query):
    query_count, width = queries.shape
    ext_rows = keys_ext.shape[0]
    rows = BLK
    block_total = query_count // rows
    first = jnp.reshape(first_query, (1,)).astype(jnp.int32)
    grid_spec = pltpu.PrefetchScalarGridSpec(
        num_scalar_prefetch=1,
        grid=(block_total,),
        in_specs=[
            pl.BlockSpec((rows, width), lambda b, f: (b, 0)),
            pl.BlockSpec((rows, width), lambda b, f: (b, 0)),
            pl.BlockSpec((ext_rows, HD), lambda b, f: (0, 0)),
            pl.BlockSpec((ext_rows, HD), lambda b, f: (0, 0)),
        ],
        out_specs=[
            pl.BlockSpec((rows, width), lambda b, f: (b, 0)),
            pl.BlockSpec((rows, width), lambda b, f: (b, 0)),
            pl.BlockSpec((ext_rows, HD), lambda b, f: (0, 0)),
            pl.BlockSpec((ext_rows, HD), lambda b, f: (0, 0)),
        ],
    )
    return pl.pallas_call(
        attend_kernel,
        grid_spec=grid_spec,
        out_shape=[
            jax.ShapeDtypeStruct((query_count, width), jnp.bfloat16),
            jax.ShapeDtypeStruct((query_count, width), jnp.bfloat16),
            jax.ShapeDtypeStruct((ext_rows, HD), jnp.float32),
            jax.ShapeDtypeStruct((ext_rows, HD), jnp.float32),
        ],
        compiler_params=pltpu.CompilerParams(
            dimension_semantics=("arbitrary",), vmem_limit_bytes=56 * 1024 * 1024
        ),
    )(first, queries, grads, keys_ext, values_ext)


def body(queries, keys, values, grad_out):
    token_count = queries.shape[0]
    query_rows = queries.reshape(token_count, QH, HD)
    key_rows = keys.reshape(token_count, KVH, HD)
    value_rows = values.reshape(token_count, KVH, HD)
    grad_rows = grad_out.reshape(token_count, QH, HD)
    group_queries, group_keys, group_values, group_grads = (
        lax.all_to_all(query_rows, "head", split_axis=1, concat_axis=0, tiled=True),
        lax.all_to_all(key_rows, "head", split_axis=1, concat_axis=0, tiled=True),
        lax.all_to_all(value_rows, "head", split_axis=1, concat_axis=0, tiled=True),
        lax.all_to_all(grad_rows, "head", split_axis=1, concat_axis=0, tiled=True),
    )
    group_rows = group_queries.shape[0]
    query_heads = group_queries.shape[1]
    first_query = lax.axis_index("ctx") * group_rows
    group_keys = group_keys.reshape(group_rows, HD)
    group_values = group_values.reshape(group_rows, HD)
    key_tail, value_tail = shifted(
        (group_keys[group_rows - WIN :], group_values[group_rows - WIN :]), "ctx", 1
    )
    keys_ext = jnp.concatenate([key_tail, group_keys], axis=0)
    values_ext = jnp.concatenate([value_tail, group_values], axis=0)
    attended_group, grad_query_group, key_total, value_total = attend(
        group_queries.reshape(group_rows, query_heads * HD),
        keys_ext,
        values_ext,
        group_grads.reshape(group_rows, query_heads * HD),
        first_query,
    )
    key_back, value_back = (
        shifted(key_total[:WIN].astype(jnp.bfloat16), "ctx", -1).astype(jnp.float32),
        shifted(value_total[:WIN].astype(jnp.bfloat16), "ctx", -1).astype(jnp.float32),
    )
    key_grad = jnp.concatenate(
        [key_total[WIN:group_rows], key_total[group_rows:] + key_back], axis=0
    ).astype(jnp.bfloat16)
    value_grad = jnp.concatenate(
        [value_total[WIN:group_rows], value_total[group_rows:] + value_back], axis=0
    ).astype(jnp.bfloat16)
    attended_group = attended_group.reshape(group_rows, query_heads, HD)
    grad_query_group = grad_query_group.reshape(group_rows, query_heads, HD)
    key_grad = key_grad.reshape(group_rows, 1, HD)
    value_grad = value_grad.reshape(group_rows, 1, HD)
    attended, grad_queries, key_out, value_out = (
        lax.all_to_all(attended_group, "head", split_axis=0, concat_axis=1, tiled=True),
        lax.all_to_all(grad_query_group, "head", split_axis=0, concat_axis=1, tiled=True),
        lax.all_to_all(key_grad, "head", split_axis=0, concat_axis=1, tiled=True),
        lax.all_to_all(value_grad, "head", split_axis=0, concat_axis=1, tiled=True),
    )
    return (
        attended.reshape(token_count, QH * HD),
        grad_queries.reshape(token_count, QH * HD),
        key_out.reshape(token_count, KVH * HD),
        value_out.reshape(token_count, KVH * HD),
    )


def solution(mesh):
    placed = (
        P(("ctx", "head"), None),
        P(("ctx", "head"), None),
        P(("ctx", "head"), None),
        P(("ctx", "head"), None),
    )
    return jax.shard_map(
        body,
        mesh=mesh,
        in_specs=placed,
        out_specs=(
            P(("ctx", "head"), None),
            P(("ctx", "head"), None),
            P(("ctx", "head"), None),
            P(("ctx", "head"), None),
        ),
        check_vma=False,
    )
```

time: 596 us -> 332 us (0.56)
  matrix products: 214 us -> 0 us
  Pallas kernels: 0 us -> 56.3 us
  local copies, waits for them, and re-layouts: 120 us -> 65.8 us
  other arithmetic: 58.2 us -> 9.75 us
  loops' own time: 11.8 us -> 0 us
  waiting for transfers between devices: 129 us -> 140 us
    dot_general x80 -> x0, matrix products: 157 us -> none  [the longest x16 38.9 us: block_step(): jnp.einsum('sgqd,skd->sgqk', grad_stack, value_stack, preferred_element_t...]
    sub x16 -> x0, matrix products: 57.1 us -> none  [block_step(): unnormed = jnp.exp(scores - largest)]
    pallas_call x0 -> x1, Pallas kernels: none -> 56.3 us  [attend(): pl.pallas_call(attend_kernel, grid_spec=grid_spec, out_shape=[jax.ShapeDt...]
    convert_element_type x16 -> x0, other arithmetic: 32.3 us -> none  [block_step(): probs_low = probs.astype(jnp.bfloat16)]
    dynamic_slice x48 -> x0, local copies, waits for them, and re-layouts: 25.9 us -> none  [the longest x32 16.6 us: block_step(): grad_stack = lax.dynamic_slice_in_dim(grad_major, first_row, block_rows, 2)]
    dynamic_update_slice x32 -> x0, local copies, waits for them, and re-layouts: 12.6 us -> none  [attend(): lax.scan(block_step, None, jnp.arange(block_total, dtype=jnp.int32))]
    squeeze x2 -> x0, local copies, waits for them, and re-layouts: 11.9 us -> none  [place_blocks(): piece = stacked[:, :, offset]]
    another operation x1 -> x0, loops' own time: 11.8 us -> none  [attend(): lax.scan(block_step, None, jnp.arange(block_total, dtype=jnp.int32))]
  transfers between devices with their start and end apart: 12 -> 12, of which waited for: 9 -> 10; matrix products, arithmetic and copies ran while one was open for 12% -> 15% of each run, Pallas kernels for 0% -> 0%
where the time goes in v1:
time: 332 us; the launch traced here: 331 us
  waiting for transfers between devices  140 us (42%)
  local copies, waits for them, and re-layouts  65.8 us (20%)
  starting transfers between devices  57.8 us (17%)
  Pallas kernels  56.3 us (17%)
  other arithmetic  9.75 us (3%)
    pallas_call x1, Pallas kernels, attend(): pl.pallas_call(attend_kernel, grid_spec=grid_spec, out_shape=[jax.ShapeDt...  56.3 us
    ppermute x4, waiting for transfers between devices, shifted(): return lax.ppermute(block, axis, route)  31.2 us
    all_to_all x1, waiting for transfers between devices, body(): lax.all_to_all(attended_group, 'head', split_axis=0, concat_axis=1, tiled...  25.3 us
    all_to_all x1, waiting for transfers between devices, body(): lax.all_to_all(query_rows, 'head', split_axis=1, concat_axis=0, tiled=True)  25.2 us
    unnamed x32, local copies, waits for them, and re-layouts  21.9 us
    all_to_all x1, waiting for transfers between devices, body(): lax.all_to_all(key_rows, 'head', split_axis=1, concat_axis=0, tiled=True)  13.7 us
    ppermute x4, starting transfers between devices, shifted(): return lax.ppermute(block, axis, route)  12.6 us
    all_to_all x1, waiting for transfers between devices, body(): lax.all_to_all(grad_query_group, 'head', split_axis=0, concat_axis=1, til...  12.1 us
  transfers between devices with their start and end apart: 12, of which 10 were waited for; matrix products, arithmetic and copies ran while one was open for 15% of the time, Pallas kernels for 0%

profile of v1, /device:TPU:121, one launch (start us, length us, event | category | flops | bytes accessed | tf_op | source)
XLA Modules:
  0.0 330.8 jit_solution(3629188216240803044)
XLA Ops:
  3.1 5.9 %all-to-all-start.2 = ((bf16[256,16,128]{2,0,1:T(8,128)(2,1)}), bf16[256,16,128]{2,0,1:T(8,128)(2,1)S(1)}, u32[]{:S(2)}, u32[]{:S(2)}) async-start(bf16[256,16,128]{2,0,1:T(8,128)(2,1)} %copy_bitcast_fusion.5), calls=%async_computation.2 | async-start | bytes 2097152 | tf_op jit(solution)/shard_map/all_to_all | solution.py:116
  10.3 13.7 %all-to-all-done.2 = bf16[256,16,128]{2,0,1:T(8,128)(2,1)S(1)} async-done(((bf16[256,16,128]{2,0,1:T(8,128)(2,1)}), bf16[256,16,128]{2,0,1:T(8,128)(2,1)S(1)}, u32[]{:S(2)}, u32[]{:S(2)}) %all-to-all-start.2) | async-done | bytes 1048608 | tf_op jit(solution)/shard_map/all_to_all | solution.py:116
  24.0 5.2 %all-to-all-start.3 = ((bf16[256,16,128]{2,0,1:T(8,128)(2,1)}), bf16[256,16,128]{2,0,1:T(8,128)(2,1)S(1)}, u32[]{:S(2)}, u32[]{:S(2)}) async-start(bf16[256,16,128]{2,0,1:T(8,128)(2,1)} %copy_bitcast_fusion.4), calls=%async_computation.3 | async-start | bytes 2097152 | tf_op jit(solution)/shard_map/all_to_all | solution.py:117
  29.1 4.1 %copy.60 = bf16[256,4096]{0,1:T(8,128)(2,1)} copy(bf16[256,4096]{1,0:T(8,128)(2,1)} %param.4) | data formatting | bytes 4194304 | tf_op args[0]
  33.2 10.9 %all-to-all-done.3 = bf16[256,16,128]{2,0,1:T(8,128)(2,1)S(1)} async-done(((bf16[256,16,128]{2,0,1:T(8,128)(2,1)}), bf16[256,16,128]{2,0,1:T(8,128)(2,1)S(1)}, u32[]{:S(2)}, u32[]{:S(2)}) %all-to-all-start.3) | async-done | bytes 1048608 | tf_op jit(solution)/shard_map/all_to_all | solution.py:117
  45.1 5.3 %all-to-all-start = ((bf16[256,32,128]{0,2,1:T(8,128)(2,1)}), bf16[256,32,128]{0,2,1:T(8,128)(2,1)S(1)}, u32[]{:S(2)}, u32[]{:S(2)}) async-start(bf16[256,32,128]{0,2,1:T(8,128)(2,1)} %bitcast.66), calls=%async_computation | async-start | bytes 4194304 | tf_op jit(solution)/shard_map/all_to_all | solution.py:115
  50.3 4.1 %copy.63 = bf16[256,4096]{0,1:T(8,128)(2,1)} copy(bf16[256,4096]{1,0:T(8,128)(2,1)} %param.7) | data formatting | bytes 4194304 | tf_op args[3]
  54.4 25.2 %all-to-all-done = bf16[256,32,128]{0,2,1:T(8,128)(2,1)S(1)} async-done(((bf16[256,32,128]{0,2,1:T(8,128)(2,1)}), bf16[256,32,128]{0,2,1:T(8,128)(2,1)S(1)}, u32[]{:S(2)}, u32[]{:S(2)}) %all-to-all-start) | async-done | bytes 2097184 | tf_op jit(solution)/shard_map/all_to_all | solution.py:115
  79.6 4.5 %all-to-all-start.1 = ((bf16[256,32,128]{0,2,1:T(8,128)(2,1)}), bf16[256,32,128]{0,2,1:T(8,128)(2,1)}, u32[]{:S(2)}, u32[]{:S(2)}) async-start(bf16[256,32,128]{0,2,1:T(8,128)(2,1)} %bitcast.64), calls=%async_computation.1 | async-start | bytes 4194304 | tf_op jit(solution)/shard_map/all_to_all | solution.py:118
  84.8 4.3 %collective-permute-start = (bf16[1024,128]{1,0:T(8,128)(2,1)}, bf16[1024,128]{1,0:T(8,128)(2,1)S(1)}, u32[]{:S(2)}, u32[]{:S(2)}) collective-permute-start(bf16[1024,128]{1,0:T(8,128)(2,1)} %bitcast.11), channel_id=1, source_target_pairs={{0,16},{16,32},{32,48},{48,64},{64,80},{80,96},{96,112},{1,17},{17... | collective-permute-start | bytes 786440 | tf_op jit(solution)/shard_map/ppermute | solution.py:21
  92.1 23.7 %collective-permute-done = bf16[1024,128]{1,0:T(8,128)(2,1)S(1)} collective-permute-done((bf16[1024,128]{1,0:T(8,128)(2,1)}, bf16[1024,128]{1,0:T(8,128)(2,1)S(1)}, u32[]{:S(2)}, u32[]{:S(2)}) %collective-permute-start) | collective-permute-done | bytes 262176 | tf_op jit(solution)/shard_map/ppermute | solution.py:21
  117.0 4.5 %collective-permute-done.1 = bf16[1024,128]{1,0:T(8,128)(2,1)S(1)} collective-permute-done((bf16[1024,128]{1,0:T(8,128)(2,1)S(1)}, bf16[1024,128]{1,0:T(8,128)(2,1)S(1)}, u32[]{:S(2)}, u32[]{:S(2)}) %collective-permute-start.1) | collective-permute-done | bytes 262176 | tf_op jit(solution)/shard_map/ppermute | solution.py:21
  122.6 3.8 %copy.62 = bf16[16,256,2,128]{3,2,1,0:T(2,128)(2,1)} copy(bf16[16,256,2,128]{1,3,2,0:T(8,128)(2,1)S(1)} %bitcast.63) | data formatting | bytes 4194304 | tf_op jit(solution)/shard_map/all_to_all | solution.py:115
  126.4 6.3 %copy.65 = bf16[16,256,2,128]{3,2,1,0:T(2,128)(2,1)} copy(bf16[16,256,2,128]{1,3,2,0:T(8,128)(2,1)} %bitcast.8) | data formatting | bytes 4194304 | tf_op jit(solution)/shard_map/all_to_all | solution.py:118
  132.7 4.4 %copy_bitcast_fusion = (bf16[4096,256]{1,0:T(8,128)(2,1)}, bf16[4096,256]{1,0:T(8,128)(2,1)}) fusion(bf16[512,8,2,128]{3,2,1,0:T(2,128)(2,1)} %bitcast.70, bf16[512,8,2,128]{3,2,1,0:T(2,128)(2,1)S(1)} %bitcast.69), kind=kLoop, calls=%fused_computation | loop fusion | bytes 8388608 | tf_op jit(solution)/shard_map/reshape | solution.py:134
  137.1 56.3 %shard_map.75 = (bf16[4096,256]{1,0:T(8,128)(2,1)}, bf16[4096,256]{1,0:T(8,128)(2,1)}, f32[5120,128]{1,0:T(8,128)}, f32[5120,128]{1,0:T(8,128)}) custom-call(s32[1]{0:T(128)} %bitcast.first_ref, bf16[4096,256]{1,0:T(8,128)(2,1)} %get-tuple-element.17.q_ref, bf16[4096,256]{1,0:T(8,128)(2,1)} %get-tuple-element.16.g_ref, ...), custom_call_target="tpu_custom_call" | custom-call | tf_op jit(solution)/shard_map/pallas_call | solution.py:93
  198.8 3.9 %collective-permute-start.2 = (bf16[1024,128]{1,0:T(8,128)(2,1)}, bf16[1024,128]{1,0:T(8,128)(2,1)}, u32[]{:S(2)}, u32[]{:S(2)}) collective-permute-start(bf16[1024,128]{1,0:T(8,128)(2,1)} %slice.47), channel_id=1, source_target_pairs={{16,0},{32,16},{48,32},{64,48},{80,64},{96,80},{112,96},{17,1},{33... | collective-permute-start | bytes 786440 | tf_op jit(solution)/shard_map/ppermute | solution.py:21
  202.7 3.0 collective-permute-done.3
  209.9 9.4 %all-to-all-start.7 = ((bf16[16,2,16384]{2,1,0:T(2,128)(2,1)}), bf16[16,2,16384]{2,1,0:T(2,128)(2,1)S(1)}, u32[]{:S(2)}, u32[]{:S(2)}) async-start(bf16[16,2,16384]{2,1,0:T(2,128)(2,1)} %reshape.144), calls=%async_computation.7 | async-start | bytes 2097152 | tf_op jit(solution)/shard_map/all_to_all | solution.py:155
  223.2 11.0 %all-to-all-done.7 = bf16[16,2,16384]{2,1,0:T(2,128)(2,1)S(1)} async-done(((bf16[16,2,16384]{2,1,0:T(2,128)(2,1)}), bf16[16,2,16384]{2,1,0:T(2,128)(2,1)S(1)}, u32[]{:S(2)}, u32[]{:S(2)}) %all-to-all-start.7) | async-done | bytes 1048608 | tf_op jit(solution)/shard_map/all_to_all | solution.py:155
  234.2 5.2 %all-to-all-start.6 = ((bf16[16,2,16384]{2,1,0:T(2,128)(2,1)}), bf16[16,2,16384]{2,1,0:T(2,128)(2,1)S(1)}, u32[]{:S(2)}, u32[]{:S(2)}) async-start(bf16[16,2,16384]{2,1,0:T(2,128)(2,1)} %reshape.142), calls=%async_computation.6 | async-start | bytes 2097152 | tf_op jit(solution)/shard_map/all_to_all | solution.py:154
  239.4 4.0 %reshape.136 = bf16[4096,2,128]{2,1,0:T(2,128)(2,1)} reshape(bf16[4096,256]{1,0:T(8,128)(2,1)} %get-tuple-element.8) | data formatting | bytes 4194304 | tf_op jit(solution)/shard_map/reshape | solution.py:147
  243.4 11.0 %all-to-all-done.6 = bf16[16,2,16384]{2,1,0:T(2,128)(2,1)S(1)} async-done(((bf16[16,2,16384]{2,1,0:T(2,128)(2,1)}), bf16[16,2,16384]{2,1,0:T(2,128)(2,1)S(1)}, u32[]{:S(2)}, u32[]{:S(2)}) %all-to-all-start.6) | async-done | bytes 1048608 | tf_op jit(solution)/shard_map/all_to_all | solution.py:154
  255.4 5.3 %all-to-all-start.4 = ((bf16[4096,2,128]{2,1,0:T(2,128)(2,1)}), bf16[4096,2,128]{2,1,0:T(2,128)(2,1)S(1)}, u32[]{:S(2)}, u32[]{:S(2)}) async-start(bf16[4096,2,128]{2,1,0:T(2,128)(2,1)} %reshape.136), calls=%async_computation.4 | async-start | bytes 4194304 | tf_op jit(solution)/shard_map/all_to_all | solution.py:152
  260.6 4.0 %reshape.138 = bf16[4096,2,128]{2,1,0:T(2,128)(2,1)} reshape(bf16[4096,256]{1,0:T(8,128)(2,1)} %get-tuple-element.9) | data formatting | bytes 4194304 | tf_op jit(solution)/shard_map/reshape | solution.py:148
  264.6 25.3 %all-to-all-done.4 = bf16[4096,2,128]{2,1,0:T(2,128)(2,1)S(1)} async-done(((bf16[4096,2,128]{2,1,0:T(2,128)(2,1)}), bf16[4096,2,128]{2,1,0:T(2,128)(2,1)S(1)}, u32[]{:S(2)}, u32[]{:S(2)}) %all-to-all-start.4) | async-done | bytes 2097184 | tf_op jit(solution)/shard_map/all_to_all | solution.py:152
  291.2 4.5 %all-to-all-start.5 = ((bf16[4096,2,128]{2,1,0:T(2,128)(2,1)}), bf16[4096,2,128]{2,1,0:T(2,128)(2,1)}, u32[]{:S(2)}, u32[]{:S(2)}) async-start(bf16[4096,2,128]{2,1,0:T(2,128)(2,1)} %reshape.138), calls=%async_computation.5 | async-start | bytes 4194304 | tf_op jit(solution)/shard_map/all_to_all | solution.py:153
  305.7 2.8 copy.91
  308.4 4.5 %reshape.137 = bf16[256,4096]{1,0:T(8,128)(2,1)} reshape(bf16[256,16,2,128]{3,2,1,0:T(2,128)(2,1)} %bitcast.67) | data formatting | bytes 4194304 | tf_op jit(solution)/shard_map/reshape | solution.py:158
  312.9 12.1 %all-to-all-done.5 = bf16[4096,2,128]{2,1,0:T(2,128)(2,1)} async-done(((bf16[4096,2,128]{2,1,0:T(2,128)(2,1)}), bf16[4096,2,128]{2,1,0:T(2,128)(2,1)}, u32[]{:S(2)}, u32[]{:S(2)}) %all-to-all-start.5) | async-done | bytes 2097184 | tf_op jit(solution)/shard_map/all_to_all | solution.py:153
  325.0 3.0 copy.90
  328.0 2.8 reshape.139
  (55 shorter events, 36.4 us)
Async XLA Ops:
  0.6 1.2 copy-start
  0.6 8.4 %copy-start.10 = (bf16[256,2048]{1,0:T(8,128)(2,1)S(1)}, bf16[256,2048]{1,0:T(8,128)(2,1)}, u32[]{:S(2)}) copy-start(bf16[256,2048]{1,0:T(8,128)(2,1)} %param.6) | copy-start | bytes 3145732
  3.1 20.9 %all-to-all-start.2 = ((bf16[256,16,128]{2,0,1:T(8,128)(2,1)}), bf16[256,16,128]{2,0,1:T(8,128)(2,1)S(1)}, u32[]{:S(2)}, u32[]{:S(2)}) async-start(bf16[256,16,128]{2,0,1:T(8,128)(2,1)} %copy_bitcast_fusion.5), calls=%async_computation.2 | async-start | bytes 2097152 | tf_op jit(solution)/shard_map/all_to_all | solution.py:116
  24.0 20.1 %all-to-all-start.3 = ((bf16[256,16,128]{2,0,1:T(8,128)(2,1)}), bf16[256,16,128]{2,0,1:T(8,128)(2,1)S(1)}, u32[]{:S(2)}, u32[]{:S(2)}) async-start(bf16[256,16,128]{2,0,1:T(8,128)(2,1)} %copy_bitcast_fusion.4), calls=%async_computation.3 | async-start | bytes 2097152 | tf_op jit(solution)/shard_map/all_to_all | solution.py:117
  44.1 1.0 copy-start.5
  45.1 34.5 %all-to-all-start = ((bf16[256,32,128]{0,2,1:T(8,128)(2,1)}), bf16[256,32,128]{0,2,1:T(8,128)(2,1)S(1)}, u32[]{:S(2)}, u32[]{:S(2)}) async-start(bf16[256,32,128]{0,2,1:T(8,128)(2,1)} %bitcast.66), calls=%async_computation | async-start | bytes 4194304 | tf_op jit(solution)/shard_map/all_to_all | solution.py:115
  79.6 46.8 %all-to-all-start.1 = ((bf16[256,32,128]{0,2,1:T(8,128)(2,1)}), bf16[256,32,128]{0,2,1:T(8,128)(2,1)}, u32[]{:S(2)}, u32[]{:S(2)}) async-start(bf16[256,32,128]{0,2,1:T(8,128)(2,1)} %bitcast.64), calls=%async_computation.1 | async-start | bytes 4194304 | tf_op jit(solution)/shard_map/all_to_all | solution.py:118
  84.8 31.1 %collective-permute-start = (bf16[1024,128]{1,0:T(8,128)(2,1)}, bf16[1024,128]{1,0:T(8,128)(2,1)S(1)}, u32[]{:S(2)}, u32[]{:S(2)}) collective-permute-start(bf16[1024,128]{1,0:T(8,128)(2,1)} %bitcast.11), channel_id=1, source_target_pairs={{0,16},{16,32},{32,48},{48,64},{64,80},{80,96},{96,112},{1,17},{17... | collective-permute-start | bytes 786440 | tf_op jit(solution)/shard_map/ppermute | solution.py:21
  89.1 32.4 %copy-start.6 = (bf16[256,16,128]{2,0,1:T(8,128)(2,1)S(1)}, bf16[256,16,128]{2,0,1:T(8,128)(2,1)}, u32[]{:S(2)}) copy-start(bf16[256,16,128]{2,0,1:T(8,128)(2,1)} %copy-done.5) | copy-start | bytes 3145732
  90.2 31.3 %collective-permute-start.1 = (bf16[1024,128]{1,0:T(8,128)(2,1)S(1)}, bf16[1024,128]{1,0:T(8,128)(2,1)S(1)}, u32[]{:S(2)}, u32[]{:S(2)}) collective-permute-start(bf16[1024,128]{1,0:T(8,128)(2,1)S(1)} %bitcast.79), channel_id=1, source_target_pairs={{0,16},{16,32},{32,48},{48,64},{64,80},{80,96},{96,112},{1,17},{17... | collective-permute-start | bytes 786440 | tf_op jit(solution)/shard_map/ppermute | solution.py:21
  126.4 6.3 %copy-start.4 = (bf16[16,256,2,128]{3,2,1,0:T(2,128)(2,1)S(1)}, bf16[16,256,2,128]{3,2,1,0:T(2,128)(2,1)}, u32[]{:S(2)}) copy-start(bf16[16,256,2,128]{3,2,1,0:T(2,128)(2,1)} %copy.62) | copy-start | bytes 6291460
  193.4 4.6 %copy-start.9 = (f32[5120,128]{1,0:T(8,128)S(1)}, f32[5120,128]{1,0:T(8,128)}, u32[]{:S(2)}) copy-start(f32[5120,128]{1,0:T(8,128)} %get-tuple-element.10) | copy-start | bytes 7864324
  195.4 10.3 %collective-permute-start.3 = (bf16[1024,128]{1,0:T(8,128)(2,1)S(1)}, bf16[1024,128]{1,0:T(8,128)(2,1)S(1)}, u32[]{:S(2)}, u32[]{:S(2)}) collective-permute-start(bf16[1024,128]{1,0:T(8,128)(2,1)S(1)} %slice.49), channel_id=1, source_target_pairs={{16,0},{32,16},{48,32},{64,48},{80,64},{96,80},{112,96},{17,1},{33... | collective-permute-start | bytes 786440 | tf_op jit(solution)/shard_map/ppermute | solution.py:21
  198.8 20.6 %collective-permute-start.2 = (bf16[1024,128]{1,0:T(8,128)(2,1)}, bf16[1024,128]{1,0:T(8,128)(2,1)}, u32[]{:S(2)}, u32[]{:S(2)}) collective-permute-start(bf16[1024,128]{1,0:T(8,128)(2,1)} %slice.47), channel_id=1, source_target_pairs={{16,0},{32,16},{48,32},{64,48},{80,64},{96,80},{112,96},{17,1},{33... | collective-permute-start | bytes 786440 | tf_op jit(solution)/shard_map/ppermute | solution.py:21
  209.9 24.3 %all-to-all-start.7 = ((bf16[16,2,16384]{2,1,0:T(2,128)(2,1)}), bf16[16,2,16384]{2,1,0:T(2,128)(2,1)S(1)}, u32[]{:S(2)}, u32[]{:S(2)}) async-start(bf16[16,2,16384]{2,1,0:T(2,128)(2,1)} %reshape.144), calls=%async_computation.7 | async-start | bytes 2097152 | tf_op jit(solution)/shard_map/all_to_all | solution.py:155
  234.2 20.2 %all-to-all-start.6 = ((bf16[16,2,16384]{2,1,0:T(2,128)(2,1)}), bf16[16,2,16384]{2,1,0:T(2,128)(2,1)S(1)}, u32[]{:S(2)}, u32[]{:S(2)}) async-start(bf16[16,2,16384]{2,1,0:T(2,128)(2,1)} %reshape.142), calls=%async_computation.6 | async-start | bytes 2097152 | tf_op jit(solution)/shard_map/all_to_all | solution.py:154
  254.4 1.0 copy-start.7
  255.4 34.5 %all-to-all-start.4 = ((bf16[4096,2,128]{2,1,0:T(2,128)(2,1)}), bf16[4096,2,128]{2,1,0:T(2,128)(2,1)S(1)}, u32[]{:S(2)}, u32[]{:S(2)}) async-start(bf16[4096,2,128]{2,1,0:T(2,128)(2,1)} %reshape.136), calls=%async_computation.4 | async-start | bytes 4194304 | tf_op jit(solution)/shard_map/all_to_all | solution.py:152
  289.9 1.3 copy-start.2
  291.2 33.8 %all-to-all-start.5 = ((bf16[4096,2,128]{2,1,0:T(2,128)(2,1)}), bf16[4096,2,128]{2,1,0:T(2,128)(2,1)}, u32[]{:S(2)}, u32[]{:S(2)}) async-start(bf16[4096,2,128]{2,1,0:T(2,128)(2,1)} %reshape.138), calls=%async_computation.5 | async-start | bytes 4194304 | tf_op jit(solution)/shard_map/all_to_all | solution.py:153
  297.9 3.0 copy-start.8
  302.1 3.6 %copy-start.3 = (bf16[4096,2,128]{2,1,0:T(2,128)(2,1)S(1)}, bf16[4096,2,128]{2,1,0:T(2,128)(2,1)}, u32[]{:S(2)}) copy-start(bf16[4096,2,128]{2,1,0:T(2,128)(2,1)} %copy-done.2) | copy-start | bytes 6291460
  328.0 2.8 copy-start.1

commit v2 on v1

v2 whole, which is shorter than its diff:
```python
import functools

import jax
import jax.numpy as jnp
from jax import lax
from jax.experimental import pallas as pl
from jax.experimental.pallas import tpu as pltpu
from jax.sharding import PartitionSpec as P

HD = 128
QH = 32
KVH = 16
WIN = 1024
QPRE = 168
BLK = 256


def shifted(block, axis, distance):
    devices = range(lax.axis_size(axis))
    route = [(i - distance, i) for i in devices if i - distance in devices]
    return lax.ppermute(block, axis, route)


def attend_kernel(first_ref, q_ref, g_ref, k_ref, v_ref, *rest):
    if len(rest) == 5:
        dk_in_ref, dv_in_ref, od_ref, dk_ref, dv_ref = rest
    else:
        dk_in_ref = dv_in_ref = None
        od_ref, dk_ref, dv_ref = rest
    block = pl.program_id(0)
    rows = q_ref.shape[0]
    span = WIN + rows
    scale = QPRE ** (-0.5)

    @pl.when(block == 0)
    def _():
        if dk_in_ref is None:
            dk_ref[...] = jnp.zeros_like(dk_ref)
            dv_ref[...] = jnp.zeros_like(dv_ref)
        else:
            dk_ref[...] = dk_in_ref[...]
            dv_ref[...] = dv_in_ref[...]

    start = pl.multiple_of(block * rows, rows)
    k_win = k_ref[pl.ds(start, span), :]
    v_win = v_ref[pl.ds(start, span), :]
    row_id = lax.broadcasted_iota(jnp.int32, (rows, span), 0)
    col_id = lax.broadcasted_iota(jnp.int32, (rows, span), 1)
    distance = row_id + WIN - col_id
    key_pos = first_ref[0] - WIN + start + col_id
    allowed = (distance >= 0) & (distance < WIN) & (key_pos >= 0)
    nt = (((1,), (1,)), ((), ()))
    tn = (((0,), (0,)), ((), ()))
    q = q_ref[...]
    g = g_ref[...]
    scores = lax.dot_general(q, k_win, nt, preferred_element_type=jnp.float32) * scale
    scores = jnp.where(allowed, scores, -jnp.inf)
    largest = jnp.max(scores, axis=-1, keepdims=True)
    unnormed = jnp.exp(scores - largest)
    probs = unnormed / jnp.sum(unnormed, axis=-1, keepdims=True)
    probs_low = probs.astype(jnp.bfloat16)
    out = jnp.dot(probs_low, v_win, preferred_element_type=jnp.float32).astype(jnp.bfloat16)
    od_ref[:, :HD] = out
    grad_probs = lax.dot_general(g, v_win, nt, preferred_element_type=jnp.float32)
    inner = jnp.sum(g.astype(jnp.float32) * out.astype(jnp.float32), axis=-1, keepdims=True)
    grad_scores = (probs * (grad_probs - inner) * scale).astype(jnp.bfloat16)
    od_ref[:, HD:] = jnp.dot(grad_scores, k_win, preferred_element_type=jnp.float32).astype(
        jnp.bfloat16
    )
    dk_ref[pl.ds(start, span), :] += lax.dot_general(
        grad_scores, q, tn, preferred_element_type=jnp.float32
    )
    dv_ref[pl.ds(start, span), :] += lax.dot_general(
        probs_low, g, tn, preferred_element_type=jnp.float32
    )


def attend(source, q_col, g_col, keys_ext, values_ext, first_query, key_acc=None, value_acc=None):
    query_count = source.shape[0]
    ext_rows = keys_ext.shape[0]
    rows = BLK
    block_total = query_count // rows
    first = jnp.reshape(first_query, (1,)).astype(jnp.int32)
    whole = pl.BlockSpec((ext_rows, HD), lambda b, f: (0, 0))
    in_specs = [
        pl.BlockSpec((rows, HD), lambda b, f: (b, q_col)),
        pl.BlockSpec((rows, HD), lambda b, f: (b, g_col)),
        whole,
        whole,
    ]
    operands = [first, source, source, keys_ext, values_ext]
    aliases = {}
    if key_acc is not None:
        in_specs += [whole, whole]
        operands += [key_acc, value_acc]
        aliases = {5: 1, 6: 2}
    grid_spec = pltpu.PrefetchScalarGridSpec(
        num_scalar_prefetch=1,
        grid=(block_total,),
        in_specs=in_specs,
        out_specs=[pl.BlockSpec((rows, 2 * HD), lambda b, f: (b, 0)), whole, whole],
    )
    return pl.pallas_call(
        attend_kernel,
        grid_spec=grid_spec,
        out_shape=[
            jax.ShapeDtypeStruct((query_count, 2 * HD), jnp.bfloat16),
            jax.ShapeDtypeStruct((ext_rows, HD), jnp.float32),
            jax.ShapeDtypeStruct((ext_rows, HD), jnp.float32),
        ],
        input_output_aliases=aliases,
        compiler_params=pltpu.CompilerParams(
            dimension_semantics=("arbitrary",), vmem_limit_bytes=56 * 1024 * 1024
        ),
    )(*operands)


def exchange_in(pieces):
    stacked = jnp.transpose(jnp.concatenate(pieces, axis=-1), (1, 0, 2))
    moved = lax.all_to_all(stacked, "head", split_axis=0, concat_axis=0, tiled=True)
    return moved.reshape(moved.shape[0] * moved.shape[1], moved.shape[2])


def exchange_out(group_block, parts):
    shared = lax.axis_size("head")
    split = group_block.reshape(shared, group_block.shape[0] // shared, group_block.shape[1])
    moved = lax.all_to_all(split, "head", split_axis=0, concat_axis=0, tiled=True)
    return jnp.transpose(moved, (1, 0, 2))


def body(queries, keys, values, grad_out):
    token_count = queries.shape[0]
    shared = KVH
    group_size = QH // KVH
    query_rows = queries.reshape(token_count, shared, group_size, HD)
    grad_rows = grad_out.reshape(token_count, shared, group_size, HD)
    key_rows = keys.reshape(token_count, shared, HD)
    value_rows = values.reshape(token_count, shared, HD)
    first_part = exchange_in(
        [key_rows, value_rows, query_rows[:, :, 0], grad_rows[:, :, 0]]
    )
    second_part = exchange_in([query_rows[:, :, 1], grad_rows[:, :, 1]])
    group_rows = first_part.shape[0]
    first_query = lax.axis_index("ctx") * group_rows
    group_keys = first_part[:, :HD]
    group_values = first_part[:, HD : 2 * HD]
    key_tail, value_tail = shifted(
        (group_keys[group_rows - WIN :], group_values[group_rows - WIN :]), "ctx", 1
    )
    keys_ext = jnp.concatenate([key_tail, group_keys], axis=0)
    values_ext = jnp.concatenate([value_tail, group_values], axis=0)
    first_out, key_acc, value_acc = attend(first_part, 2, 3, keys_ext, values_ext, first_query)
    second_out, key_total, value_total = attend(
        second_part, 0, 1, keys_ext, values_ext, first_query, key_acc, value_acc
    )
    key_back, value_back = (
        shifted(key_total[:WIN].astype(jnp.bfloat16), "ctx", -1).astype(jnp.float32),
        shifted(value_total[:WIN].astype(jnp.bfloat16), "ctx", -1).astype(jnp.float32),
    )
    key_grad = jnp.concatenate(
        [key_total[WIN:group_rows], key_total[group_rows:] + key_back], axis=0
    ).astype(jnp.bfloat16)
    value_grad = jnp.concatenate(
        [value_total[WIN:group_rows], value_total[group_rows:] + value_back], axis=0
    ).astype(jnp.bfloat16)
    first_back = exchange_out(first_out, 2)
    second_back = exchange_out(jnp.concatenate([second_out, key_grad, value_grad], axis=1), 4)
    attended = jnp.stack([first_back[:, :, :HD], second_back[:, :, :HD]], axis=2)
    grad_queries = jnp.stack([first_back[:, :, HD:], second_back[:, :, HD : 2 * HD]], axis=2)
    return (
        attended.reshape(token_count, QH * HD),
        grad_queries.reshape(token_count, QH * HD),
        second_back[:, :, 2 * HD : 3 * HD].reshape(token_count, KVH * HD),
        second_back[:, :, 3 * HD :].reshape(token_count, KVH * HD),
    )


def solution(mesh):
    placed = (
        P(("ctx", "head"), None),
        P(("ctx", "head"), None),
        P(("ctx", "head"), None),
        P(("ctx", "head"), None),
    )
    return jax.shard_map(
        body,
        mesh=mesh,
        in_specs=placed,
        out_specs=(
            P(("ctx", "head"), None),
            P(("ctx", "head"), None),
            P(("ctx", "head"), None),
            P(("ctx", "head"), None),
        ),
        check_vma=False,
    )
```

time: 332 us -> 325 us (0.979)
  local copies, waits for them, and re-layouts: 65.8 us -> 44.9 us
  starting transfers between devices: 57.8 us -> 38.6 us
  waiting for transfers between devices: 140 us -> 152 us
  other arithmetic: 9.75 us -> 20.1 us
  Pallas kernels: 56.3 us -> 66.4 us
    all_to_all x8 -> x4, starting transfers between devices: 45.2 us -> 25.8 us  [the longest x2 13.8 us: exchange_out(): lax.all_to_all(split, 'head', split_axis=0, concat_axis=0, tiled=True)]
    all_to_all x6 -> x0, local copies, waits for them, and re-layouts: 18.7 us -> none  [the longest x1 6.3 us: body(): lax.all_to_all(grad_rows, 'head', split_axis=1, concat_axis=0, tiled=True)]
    unnamed x32 -> x17, local copies, waits for them, and re-layouts: 21.9 us -> 5.04 us
    slice x1 -> x6, local copies, waits for them, and re-layouts: 0.72 us -> 12 us  [the longest x1 6.51 us: body(): grad_rows[:, :, 0]]
    pallas_call x1 -> x2, Pallas kernels: 56.3 us -> 66.4 us  [attend(): pl.pallas_call(attend_kernel, grid_spec=grid_spec, out_shape=[jax.ShapeDt...]
    all_to_all x8 -> x4, waiting for transfers between devices: 109 us -> 116 us  [the longest x2 59.6 us: exchange_out(): lax.all_to_all(split, 'head', split_axis=0, concat_axis=0, tiled=True)]
    another operation x0 -> x3, local copies, waits for them, and re-layouts: none -> 6.04 us  [the longest x2 3.88 us: body(): jnp.stack([first_back[:, :, HD:], second_back[:, :, HD:2 * HD]], axis=2)]
    ppermute x4, waiting for transfers between devices: 31.2 us -> 36 us  [shifted(): return lax.ppermute(block, axis, route)]
  transfers between devices with their start and end apart: 12 -> 8, of which waited for: 10 -> 6; matrix products, arithmetic and copies ran while one was open for 15% -> 7% of each run, Pallas kernels for 0% -> 21%
where the time goes in v2:
time: 325 us; the launch traced here: 323 us
  waiting for transfers between devices  152 us (47%)
  Pallas kernels  66.4 us (20%)
  local copies, waits for them, and re-layouts  44.9 us (14%)
  starting transfers between devices  38.6 us (12%)
  other arithmetic  20.1 us (6%)
    pallas_call x2, Pallas kernels, attend(): pl.pallas_call(attend_kernel, grid_spec=grid_spec, out_shape=[jax.ShapeDt...  66.4 us
    all_to_all x2, waiting for transfers between devices, exchange_out(): lax.all_to_all(split, 'head', split_axis=0, concat_axis=0, tiled=True)  59.6 us
    all_to_all x2, waiting for transfers between devices, exchange_in(): lax.all_to_all(stacked, 'head', split_axis=0, concat_axis=0, tiled=True)  56.8 us
    ppermute x4, waiting for transfers between devices, shifted(): return lax.ppermute(block, axis, route)  36 us
    all_to_all x2, starting transfers between devices, exchange_out(): lax.all_to_all(split, 'head', split_axis=0, concat_axis=0, tiled=True)  13.8 us
    ppermute x4, starting transfers between devices, shifted(): return lax.ppermute(block, axis, route)  12.8 us
    all_to_all x2, starting transfers between devices, exchange_in(): lax.all_to_all(stacked, 'head', split_axis=0, concat_axis=0, tiled=True)  12 us
    concatenate x1, other arithmetic, body(): jnp.concatenate([second_out, key_grad, value_grad], axis=1)  8.92 us
  transfers between devices with their start and end apart: 8, of which 6 were waited for; matrix products, arithmetic and copies ran while one was open for 7% of the time, Pallas kernels for 21%

profile of v2, /device:TPU:121, one launch (start us, length us, event | category | flops | bytes accessed | tf_op | source)
XLA Modules:
  0.0 323.3 jit_solution(1325460393712980216)
XLA Ops:
  0.6 3.3 %reshape.51 = bf16[256,16,2,128]{3,2,1,0:T(2,128)(2,1)S(1)} reshape(bf16[256,4096]{1,0:T(8,128)(2,1)} %param.4) | data formatting | bytes 4194304 | tf_op jit(solution)/shard_map/reshape | solution.py:135
  4.0 4.4 %reshape.52 = bf16[256,16,2,128]{3,2,1,0:T(2,128)(2,1)} reshape(bf16[256,4096]{1,0:T(8,128)(2,1)} %param.7) | data formatting | bytes 4194304 | tf_op jit(solution)/shard_map/reshape | solution.py:136
  8.4 6.5 %fusion.3 = (bf16[256,16,1,128]{3,2,1,0:T(2,128)(2,1)S(1)}, bf16[256,16,1,128]{3,2,1,0:T(2,128)(2,1)}) fusion(bf16[256,16,2,128]{3,2,1,0:T(2,128)(2,1)} %reshape.52), kind=kLoop, calls=%fused_computation.26 | loop fusion | bytes 4194304 | tf_op jit(solution)/shard_map/slice | solution.py:140
  14.9 3.8 %fusion.2 = (bf16[256,16,1,128]{3,2,1,0:T(2,128)(2,1)S(1)}, bf16[256,16,1,128]{3,2,1,0:T(2,128)(2,1)}) fusion(bf16[256,16,2,128]{3,2,1,0:T(2,128)(2,1)S(1)} %reshape.51), kind=kLoop, calls=%fused_computation.25 | loop fusion | bytes 4194304 | tf_op jit(solution)/shard_map/slice | solution.py:140
  20.6 2.3 maximum_bitcast_fusion
  23.0 6.0 %all-to-all-start = ((bf16[16,256,512]{2,1,0:T(8,128)(2,1)}), bf16[16,256,512]{2,1,0:T(8,128)(2,1)}, u32[]{:S(2)}, u32[]{:S(2)}) async-start(bf16[16,256,512]{2,1,0:T(8,128)(2,1)} %maximum_bitcast_fusion), calls=%async_computation | async-start | bytes 8388608 | tf_op jit(solution)/shard_map/all_to_all | solution.py:120
  29.0 2.9 copy_bitcast_fusion.4
  32.0 1.6 maximum_bitcast_fusion.1
  33.6 56.8 %all-to-all-done = bf16[16,256,512]{2,1,0:T(8,128)(2,1)} async-done(((bf16[16,256,512]{2,1,0:T(8,128)(2,1)}), bf16[16,256,512]{2,1,0:T(8,128)(2,1)}, u32[]{:S(2)}, u32[]{:S(2)}) %all-to-all-start) | async-done | bytes 4194336 | tf_op jit(solution)/shard_map/all_to_all | solution.py:120
  90.3 5.9 %all-to-all-start.2 = ((bf16[16,256,256]{2,1,0:T(8,128)(2,1)}), bf16[16,256,256]{2,1,0:T(8,128)(2,1)S(1)}, u32[]{:S(2)}, u32[]{:S(2)}) async-start(bf16[16,256,256]{2,1,0:T(8,128)(2,1)} %maximum_bitcast_fusion.1), calls=%async_computation.2 | async-start | bytes 4194304 | tf_op jit(solution)/shard_map/all_to_all | solution.py:120
  97.4 4.4 %collective-permute-start.1 = (bf16[1024,128]{1,0:T(8,128)(2,1)S(1)}, bf16[1024,128]{1,0:T(8,128)(2,1)S(1)}, u32[]{:S(2)}, u32[]{:S(2)}) collective-permute-start(bf16[1024,128]{1,0:T(8,128)(2,1)S(1)} %get-tuple-element.20), channel_id=1, source_target_pairs={{0,16},{16,32},{32,48},{48,64},{64,80},{80,96},{96,112},{1,17},{17... | collective-permute-start | bytes 786440 | tf_op jit(solution)/shard_map/ppermute | solution.py:21
  101.7 1.7 fusion.1
  103.4 1.9 collective-permute-start
  105.4 22.8 %collective-permute-done.1 = bf16[1024,128]{1,0:T(8,128)(2,1)S(1)} collective-permute-done((bf16[1024,128]{1,0:T(8,128)(2,1)S(1)}, bf16[1024,128]{1,0:T(8,128)(2,1)S(1)}, u32[]{:S(2)}, u32[]{:S(2)}) %collective-permute-start.1) | collective-permute-done | bytes 262176 | tf_op jit(solution)/shard_map/ppermute | solution.py:21
  129.3 4.5 %collective-permute-done = bf16[1024,128]{1,0:T(8,128)(2,1)S(1)} collective-permute-done((bf16[1024,128]{1,0:T(8,128)(2,1)S(1)}, bf16[1024,128]{1,0:T(8,128)(2,1)S(1)}, u32[]{:S(2)}, u32[]{:S(2)}) %collective-permute-start) | collective-permute-done | bytes 262176 | tf_op jit(solution)/shard_map/ppermute | solution.py:21
  134.9 32.4 %shard_map.75 = (bf16[4096,256]{1,0:T(8,128)(2,1)}, f32[5120,128]{1,0:T(8,128)}, f32[5120,128]{1,0:T(8,128)}) custom-call(s32[1]{0:T(128)} %bitcast.first_ref, bf16[4096,512]{1,0:T(8,128)(2,1)} %bitcast.4.q_ref.g_ref, bf16[4096,512]{1,0:T(8,128)(2,1)} %bitcast.4.q_ref.g_ref, bf16[5120,128]{1,0:T(8,128)(2,1)} %pad_maximum_fusion.2.k_ref, ...), custom_call_target="tpu_custom_call" | custom-call | tf_op jit(solution)/shard_map/pallas_call | solution.py:103
  168.6 7.2 %all-to-all-start.1 = ((bf16[16,256,256]{2,1,0:T(8,128)(2,1)}), bf16[16,256,256]{2,1,0:T(8,128)(2,1)}, u32[]{:S(2)}, u32[]{:S(2)}) async-start(bf16[16,256,256]{2,1,0:T(8,128)(2,1)} %bitcast.50), calls=%async_computation.1 | async-start | bytes 4194304 | tf_op jit(solution)/shard_map/all_to_all | solution.py:127
  175.9 34.0 %shard_map.76 = (bf16[4096,256]{1,0:T(8,128)(2,1)}, f32[5120,128]{1,0:T(8,128)}, f32[5120,128]{1,0:T(8,128)}) custom-call(s32[1]{0:T(128)} %bitcast.first_ref, bf16[4096,256]{1,0:T(8,128)(2,1)} %bitcast.47, bf16[4096,256]{1,0:T(8,128)(2,1)} %bitcast.48, bf16[5120,128]{1,0:T(8,128)(2,1)} %pad_maximum_fusion.2.k_ref, ...), custom_call_target="tpu_custom_call", output_to_operand_aliasing={{1}: (5, {}), {2}: (6, {})} | custom-call | tf_op jit(solution)/shard_map/pallas_call | solution.py:103
  209.9 2.0 convert.16
  212.0 3.7 %collective-permute-start.2 = (bf16[1024,128]{1,0:T(8,128)(2,1)S(1)}, bf16[1024,128]{1,0:T(8,128)(2,1)S(1)}, u32[]{:S(2)}, u32[]{:S(2)}) collective-permute-start(bf16[1024,128]{1,0:T(8,128)(2,1)S(1)} %slice.96), channel_id=1, source_target_pairs={{16,0},{32,16},{48,32},{64,48},{80,64},{96,80},{112,96},{17,1},{33... | collective-permute-start | bytes 786440 | tf_op jit(solution)/shard_map/ppermute | solution.py:21
  215.8 2.8 collective-permute-start.3
  218.8 4.2 %collective-permute-done.2 = bf16[1024,128]{1,0:T(8,128)(2,1)S(1)} collective-permute-done((bf16[1024,128]{1,0:T(8,128)(2,1)S(1)}, bf16[1024,128]{1,0:T(8,128)(2,1)S(1)}, u32[]{:S(2)}, u32[]{:S(2)}) %collective-permute-start.2) | collective-permute-done | bytes 262176 | tf_op jit(solution)/shard_map/ppermute | solution.py:21
  224.1 4.5 %collective-permute-done.3 = bf16[1024,128]{1,0:T(8,128)(2,1)S(1)} collective-permute-done((bf16[1024,128]{1,0:T(8,128)(2,1)S(1)}, bf16[1024,128]{1,0:T(8,128)(2,1)S(1)}, u32[]{:S(2)}, u32[]{:S(2)}) %collective-permute-start.3) | collective-permute-done | bytes 262176 | tf_op jit(solution)/shard_map/ppermute | solution.py:21
  228.7 8.9 %maximum_maximum_fusion = bf16[4096,512]{1,0:T(8,128)(2,1)} fusion(bf16[1024,128]{1,0:T(8,128)(2,1)S(1)} %add_convert_fusion, bf16[3072,128]{1,0:T(8,128)(2,1)S(1)} %slice.97, bf16[1024,128]{1,0:T(8,128)(2,1)S(1)} %add_convert_fusion.1, bf16[3072,128]{1,0:T(8,128)(2,1)S(1)} %slice-done, bf16[4096,256]{1,0:T(8,128)(2,1)S(1)} %copy-done.6), kind=kLoop, calls=%fused_computation.1 | loop fusion | flops 20971520 | bytes 8388608 | tf_op jit(solution)/shard_map/concatenate | solution.py:167
  237.6 6.6 %all-to-all-start.3 = ((bf16[16,256,512]{2,1,0:T(8,128)(2,1)}), bf16[16,256,512]{2,1,0:T(8,128)(2,1)}, u32[]{:S(2)}, u32[]{:S(2)}) async-start(bf16[16,256,512]{2,1,0:T(8,128)(2,1)} %bitcast.49), calls=%async_computation.3 | async-start | bytes 8388608 | tf_op jit(solution)/shard_map/all_to_all | solution.py:127
  244.2 1.7 slice_bitcast_fusion.3
  245.9 59.6 %all-to-all-done.3 = bf16[16,256,512]{2,1,0:T(8,128)(2,1)} async-done(((bf16[16,256,512]{2,1,0:T(8,128)(2,1)}), bf16[16,256,512]{2,1,0:T(8,128)(2,1)}, u32[]{:S(2)}, u32[]{:S(2)}) %all-to-all-start.3) | async-done | bytes 4194336 | tf_op jit(solution)/shard_map/all_to_all | solution.py:127
  305.5 3.7 %slice_bitcast_fusion = (bf16[16,32,8,128]{3,2,1,0:T(8,128)(2,1)S(1)}, bf16[16,32,8,128]{3,2,1,0:T(8,128)(2,1)S(1)}, bf16[256,16,1,128]{3,0,1,2:T(8,128)(2,1)S(1)}, bf16[256,16,1,128]{3,0,1,2:T(8,128)(2,1)}) fusion(bf16[256,16,512]{2,0,1:T(8,128)(2,1)} %bitcast.13), kind=kLoop, calls=%fused_computation.11 | loop fusion | bytes 8388608
  311.9 2.2 copy.17
  314.1 2.8 reshape.58
  318.3 2.2 copy.16
  320.5 2.8 reshape.57
  (35 shorter events, 12.2 us)
Async XLA Ops:
  0.6 19.4 %copy-start = (bf16[256,2048]{1,0:T(8,128)(2,1)S(1)}, bf16[256,2048]{1,0:T(8,128)(2,1)}, u32[]{:S(2)}) copy-start(bf16[256,2048]{1,0:T(8,128)(2,1)} %param.5) | copy-start | bytes 3145732
  18.7 1.4 copy-start.7
  22.9 6.1 %copy-start.4 = (bf16[256,16,1,128]{3,2,1,0:T(2,128)(2,1)S(1)}, bf16[256,16,1,128]{3,2,1,0:T(2,128)(2,1)}, u32[]{:S(2)}) copy-start(bf16[256,16,1,128]{3,2,1,0:T(2,128)(2,1)} %get-tuple-element.29) | copy-start | bytes 3145732
  23.0 67.4 %all-to-all-start = ((bf16[16,256,512]{2,1,0:T(8,128)(2,1)}), bf16[16,256,512]{2,1,0:T(8,128)(2,1)}, u32[]{:S(2)}, u32[]{:S(2)}) async-start(bf16[16,256,512]{2,1,0:T(8,128)(2,1)} %maximum_bitcast_fusion), calls=%async_computation | async-start | bytes 8388608 | tf_op jit(solution)/shard_map/all_to_all | solution.py:120
  90.3 77.0 %all-to-all-start.2 = ((bf16[16,256,256]{2,1,0:T(8,128)(2,1)}), bf16[16,256,256]{2,1,0:T(8,128)(2,1)S(1)}, u32[]{:S(2)}, u32[]{:S(2)}) async-start(bf16[16,256,256]{2,1,0:T(8,128)(2,1)} %maximum_bitcast_fusion.1), calls=%async_computation.2 | async-start | bytes 4194304 | tf_op jit(solution)/shard_map/all_to_all | solution.py:120
  97.4 30.7 %collective-permute-start.1 = (bf16[1024,128]{1,0:T(8,128)(2,1)S(1)}, bf16[1024,128]{1,0:T(8,128)(2,1)S(1)}, u32[]{:S(2)}, u32[]{:S(2)}) collective-permute-start(bf16[1024,128]{1,0:T(8,128)(2,1)S(1)} %get-tuple-element.20), channel_id=1, source_target_pairs={{0,16},{16,32},{32,48},{48,64},{64,80},{80,96},{96,112},{1,17},{17... | collective-permute-start | bytes 786440 | tf_op jit(solution)/shard_map/ppermute | solution.py:21
  103.4 30.3 %collective-permute-start = (bf16[1024,128]{1,0:T(8,128)(2,1)S(1)}, bf16[1024,128]{1,0:T(8,128)(2,1)S(1)}, u32[]{:S(2)}, u32[]{:S(2)}) collective-permute-start(bf16[1024,128]{1,0:T(8,128)(2,1)S(1)} %get-tuple-element.21), channel_id=1, source_target_pairs={{0,16},{16,32},{32,48},{48,64},{64,80},{80,96},{96,112},{1,17},{17... | collective-permute-start | bytes 786440 | tf_op jit(solution)/shard_map/ppermute | solution.py:21
  167.3 1.3 copy-start.2
  168.6 69.0 %all-to-all-start.1 = ((bf16[16,256,256]{2,1,0:T(8,128)(2,1)}), bf16[16,256,256]{2,1,0:T(8,128)(2,1)}, u32[]{:S(2)}, u32[]{:S(2)}) async-start(bf16[16,256,256]{2,1,0:T(8,128)(2,1)} %bitcast.50), calls=%async_computation.1 | async-start | bytes 4194304 | tf_op jit(solution)/shard_map/all_to_all | solution.py:127
  209.9 5.8 %copy-start.3 = (f32[5120,128]{1,0:T(8,128)S(1)}, f32[5120,128]{1,0:T(8,128)}, u32[]{:S(2)}) copy-start(f32[5120,128]{1,0:T(8,128)} %get-tuple-element.15) | copy-start | bytes 7864324
  211.9 6.8 %copy-start.5 = (bf16[5120,128]{1,0:T(8,128)(2,1)}, bf16[5120,128]{1,0:T(8,128)(2,1)S(1)}, u32[]{:S(2)}) copy-start(bf16[5120,128]{1,0:T(8,128)(2,1)S(1)} %convert.16) | copy-start | bytes 3932164
  212.0 11.0 %collective-permute-start.2 = (bf16[1024,128]{1,0:T(8,128)(2,1)S(1)}, bf16[1024,128]{1,0:T(8,128)(2,1)S(1)}, u32[]{:S(2)}, u32[]{:S(2)}) collective-permute-start(bf16[1024,128]{1,0:T(8,128)(2,1)S(1)} %slice.96), channel_id=1, source_target_pairs={{16,0},{32,16},{48,32},{64,48},{80,64},{96,80},{112,96},{17,1},{33... | collective-permute-start | bytes 786440 | tf_op jit(solution)/shard_map/ppermute | solution.py:21
  215.8 12.8 %collective-permute-start.3 = (bf16[1024,128]{1,0:T(8,128)(2,1)S(1)}, bf16[1024,128]{1,0:T(8,128)(2,1)S(1)}, u32[]{:S(2)}, u32[]{:S(2)}) collective-permute-start(bf16[1024,128]{1,0:T(8,128)(2,1)S(1)} %slice.98), channel_id=1, source_target_pairs={{16,0},{32,16},{48,32},{64,48},{80,64},{96,80},{112,96},{17,1},{33... | collective-permute-start | bytes 786440 | tf_op jit(solution)/shard_map/ppermute | solution.py:21
  218.7 10.0 %slice-start = ((bf16[5120,128]{1,0:T(8,128)(2,1)}), bf16[3072,128]{1,0:T(8,128)(2,1)S(1)}, s32[]{:S(2)}) async-start(bf16[5120,128]{1,0:T(8,128)(2,1)} %copy-done.5), calls=%async_computation.4 | async-start | bytes 1572864 | tf_op jit(solution)/shard_map/slice | solution.py:161
  218.7 10.0 %copy-start.6 = (bf16[4096,256]{1,0:T(8,128)(2,1)S(1)}, bf16[4096,256]{1,0:T(8,128)(2,1)}, u32[]{:S(2)}) copy-start(bf16[4096,256]{1,0:T(8,128)(2,1)} %get-tuple-element.13) | copy-start | bytes 6291460
  237.6 67.9 %all-to-all-start.3 = ((bf16[16,256,512]{2,1,0:T(8,128)(2,1)}), bf16[16,256,512]{2,1,0:T(8,128)(2,1)}, u32[]{:S(2)}, u32[]{:S(2)}) async-start(bf16[16,256,512]{2,1,0:T(8,128)(2,1)} %bitcast.49), calls=%async_computation.3 | async-start | bytes 8388608 | tf_op jit(solution)/shard_map/all_to_all | solution.py:127
  318.3 5.0 %copy-start.1 = (bf16[256,2048]{1,0:T(8,128)(2,1)S(1)}, bf16[256,2048]{1,0:T(8,128)(2,1)}, u32[]{:S(2)}) copy-start(bf16[256,2048]{1,0:T(8,128)(2,1)} %param.5) | copy-start | bytes 3145732

commit v3 on v2

--- a/solution.py
+++ b/solution.py
@@ -21,29 +21,30 @@
     return lax.ppermute(block, axis, route)
 
 
-def attend_kernel(first_ref, q_ref, g_ref, k_ref, v_ref, *rest):
-    if len(rest) == 5:
-        dk_in_ref, dv_in_ref, od_ref, dk_ref, dv_ref = rest
+def attend_kernel(first_ref, q_ref, g_ref, k_ref, v_ref, *rest, block_offset, key_shift, carry):
+    if carry:
+        _, dk_in_ref, dv_in_ref, od_ref, dk_ref, dv_ref = rest
     else:
-        dk_in_ref = dv_in_ref = None
         od_ref, dk_ref, dv_ref = rest
-    block = pl.program_id(0)
+    step = pl.program_id(0)
+    block = step + block_offset
     rows = q_ref.shape[0]
     span = WIN + rows
     scale = QPRE ** (-0.5)
 
-    @pl.when(block == 0)
+    @pl.when(step == 0)
     def _():
-        if dk_in_ref is None:
+        if carry:
+            dk_ref[...] = dk_in_ref[...]
+            dv_ref[...] = dv_in_ref[...]
+        else:
             dk_ref[...] = jnp.zeros_like(dk_ref)
             dv_ref[...] = jnp.zeros_like(dv_ref)
-        else:
-            dk_ref[...] = dk_in_ref[...]
-            dv_ref[...] = dv_in_ref[...]
 
     start = pl.multiple_of(block * rows, rows)
-    k_win = k_ref[pl.ds(start, span), :]
-    v_win = v_ref[pl.ds(start, span), :]
+    key_start = pl.multiple_of(block * rows - key_shift, rows)
+    k_win = k_ref[pl.ds(key_start, span), :]
+    v_win = v_ref[pl.ds(key_start, span), :]
     row_id = lax.broadcasted_iota(jnp.int32, (rows, span), 0)
     col_id = lax.broadcasted_iota(jnp.int32, (rows, span), 1)
     distance = row_id + WIN - col_id
@@ -75,33 +76,41 @@
     )
 
 
-def attend(source, q_col, g_col, keys_ext, values_ext, first_query, key_acc=None, value_acc=None):
+def attend(source, q_col, g_col, keys, values, first_query, blocks, key_shift, carried=None):
     query_count = source.shape[0]
-    ext_rows = keys_ext.shape[0]
+    ext_rows = WIN + query_count
     rows = BLK
-    block_total = query_count // rows
+    block_offset, block_count = blocks
     first = jnp.reshape(first_query, (1,)).astype(jnp.int32)
+    key_spec = pl.BlockSpec(keys.shape, lambda b, f: (0, 0))
     whole = pl.BlockSpec((ext_rows, HD), lambda b, f: (0, 0))
     in_specs = [
-        pl.BlockSpec((rows, HD), lambda b, f: (b, q_col)),
-        pl.BlockSpec((rows, HD), lambda b, f: (b, g_col)),
-        whole,
-        whole,
+        pl.BlockSpec((rows, HD), lambda b, f: (b + block_offset, q_col)),
+        pl.BlockSpec((rows, HD), lambda b, f: (b + block_offset, g_col)),
+        key_spec,
+        key_spec,
     ]
-    operands = [first, source, source, keys_ext, values_ext]
+    operands = [first, source, source, keys, values]
     aliases = {}
-    if key_acc is not None:
-        in_specs += [whole, whole]
-        operands += [key_acc, value_acc]
-        aliases = {5: 1, 6: 2}
+    if carried is not None:
+        in_specs += [pl.BlockSpec(memory_space=pl.ANY), whole, whole]
+        operands += list(carried)
+        aliases = {5: 0, 6: 1, 7: 2}
     grid_spec = pltpu.PrefetchScalarGridSpec(
         num_scalar_prefetch=1,
-        grid=(block_total,),
+        grid=(block_count,),
         in_specs=in_specs,
-        out_specs=[pl.BlockSpec((rows, 2 * HD), lambda b, f: (b, 0)), whole, whole],
+        out_specs=[
+            pl.BlockSpec((rows, 2 * HD), lambda b, f: (b + block_offset, 0)),
+            whole,
+            whole,
+        ],
+    )
+    kernel = functools.partial(
+        attend_kernel, block_offset=block_offset, key_shift=key_shift, carry=carried is not None
     )
     return pl.pallas_call(
-        attend_kernel,
+        kernel,
         grid_spec=grid_spec,
         out_shape=[
             jax.ShapeDtypeStruct((query_count, 2 * HD), jnp.bfloat16),
@@ -121,7 +130,7 @@
     return moved.reshape(moved.shape[0] * moved.shape[1], moved.shape[2])
 
 
-def exchange_out(group_block, parts):
+def exchange_out(group_block):
     shared = lax.axis_size("head")
     split = group_block.reshape(shared, group_block.shape[0] // shared, group_block.shape[1])
     moved = lax.all_to_all(split, "head", split_axis=0, concat_axis=0, tiled=True)
@@ -131,31 +140,42 @@
 def body(queries, keys, values, grad_out):
     token_count = queries.shape[0]
     shared = KVH
-    group_size = QH // KVH
-    query_rows = queries.reshape(token_count, shared, group_size, HD)
-    grad_rows = grad_out.reshape(token_count, shared, group_size, HD)
+    pair = (QH // KVH) * HD
+    query_rows = queries.reshape(token_count, shared, pair)
+    grad_rows = grad_out.reshape(token_count, shared, pair)
     key_rows = keys.reshape(token_count, shared, HD)
     value_rows = values.reshape(token_count, shared, HD)
     first_part = exchange_in(
-        [key_rows, value_rows, query_rows[:, :, 0], grad_rows[:, :, 0]]
-    )
-    second_part = exchange_in([query_rows[:, :, 1], grad_rows[:, :, 1]])
+        [key_rows, value_rows, query_rows[:, :, :HD], grad_rows[:, :, :HD]]
+    )
+    second_part = exchange_in([query_rows[:, :, HD:], grad_rows[:, :, HD:]])
     group_rows = first_part.shape[0]
+    block_total = group_rows // BLK
+    lead = WIN // BLK
     first_query = lax.axis_index("ctx") * group_rows
     group_keys = first_part[:, :HD]
     group_values = first_part[:, HD : 2 * HD]
     key_tail, value_tail = shifted(
         (group_keys[group_rows - WIN :], group_values[group_rows - WIN :]), "ctx", 1
     )
+    late = (lead, block_total - lead)
+    early = (0, lead)
+    carried = attend(first_part, 2, 3, group_keys, group_values, first_query, late, WIN)
     keys_ext = jnp.concatenate([key_tail, group_keys], axis=0)
     values_ext = jnp.concatenate([value_tail, group_values], axis=0)
-    first_out, key_acc, value_acc = attend(first_part, 2, 3, keys_ext, values_ext, first_query)
+    first_out, key_acc, value_acc = attend(
+        first_part, 2, 3, keys_ext, values_ext, first_query, early, 0, carried
+    )
+    carried = attend(
+        second_part, 0, 1, keys_ext, values_ext, first_query, early, 0,
+        (jnp.zeros_like(first_out), key_acc, value_acc),
+    )
+    key_back, value_back = (
+        shifted(carried[1][:WIN].astype(jnp.bfloat16), "ctx", -1).astype(jnp.float32),
+        shifted(carried[2][:WIN].astype(jnp.bfloat16), "ctx", -1).astype(jnp.float32),
+    )
     second_out, key_total, value_total = attend(
-        second_part, 0, 1, keys_ext, values_ext, first_query, key_acc, value_acc
-    )
-    key_back, value_back = (
-        shifted(key_total[:WIN].astype(jnp.bfloat16), "ctx", -1).astype(jnp.float32),
-        shifted(value_total[:WIN].astype(jnp.bfloat16), "ctx", -1).astype(jnp.float32),
+        second_part, 0, 1, keys_ext, values_ext, first_query, late, 0, carried
     )
     key_grad = jnp.concatenate(
         [key_total[WIN:group_rows], key_total[group_rows:] + key_back], axis=0
@@ -163,10 +183,12 @@
     value_grad = jnp.concatenate(
         [value_total[WIN:group_rows], value_total[group_rows:] + value_back], axis=0
     ).astype(jnp.bfloat16)
-    first_back = exchange_out(first_out, 2)
-    second_back = exchange_out(jnp.concatenate([second_out, key_grad, value_grad], axis=1), 4)
-    attended = jnp.stack([first_back[:, :, :HD], second_back[:, :, :HD]], axis=2)
-    grad_queries = jnp.stack([first_back[:, :, HD:], second_back[:, :, HD : 2 * HD]], axis=2)
+    first_back = exchange_out(first_out)
+    second_back = exchange_out(jnp.concatenate([second_out, key_grad, value_grad], axis=1))
+    attended = jnp.concatenate([first_back[:, :, :HD], second_back[:, :, :HD]], axis=2)
+    grad_queries = jnp.concatenate(
+        [first_back[:, :, HD:], second_back[:, :, HD : 2 * HD]], axis=2
+    )
     return (
         attended.reshape(token_count, QH * HD),
         grad_queries.reshape(token_count, QH * HD),

time: 325 us -> 285 us (0.88)
  waiting for transfers between devices: 152 us -> 119 us
  local copies, waits for them, and re-layouts: 44.9 us -> 27.8 us
  Pallas kernels: 66.4 us -> 78.7 us
    ppermute x4, waiting for transfers between devices: 36 us -> 0.43 us  [shifted(): return lax.ppermute(block, axis, route)]
    pallas_call x2 -> x4, Pallas kernels: 66.4 us -> 78.7 us  [attend(): pl.pallas_call(kernel, grid_spec=grid_spec, out_shape=[jax.ShapeDtypeStru...]
    reshape x2 -> x0, local copies, waits for them, and re-layouts: 7.75 us -> none  [the longest x1 4.43 us: body(): grad_rows = grad_out.reshape(token_count, shared, group_size, HD)]
    another operation x3 -> x0, local copies, waits for them, and re-layouts: 6.04 us -> none  [the longest x2 3.88 us: body(): jnp.stack([first_back[:, :, HD:], second_back[:, :, HD:2 * HD]], axis=2)]
    slice x4 -> x5, local copies, waits for them, and re-layouts: 10.3 us -> 4.58 us  [the longest x1 1.72 us: body(): first_back[:, :, HD:]]
    squeeze x2 -> x0, local copies, waits for them, and re-layouts: 4.3 us -> none  [the longest x1 2.95 us: body(): second_part = exchange_in([query_rows[:, :, 1], grad_rows[:, :, 1]])]
    unnamed x17 -> x23, local copies, waits for them, and re-layouts: 5.04 us -> 8.35 us
  transfers between devices with their start and end apart: 8 -> 8, of which waited for: 6 -> 3; matrix products, arithmetic and copies ran while one was open for 7% -> 10% of each run, Pallas kernels for 21% -> 28%
where the time goes in v3:
time: 285 us; the launch traced here: 283 us
  waiting for transfers between devices  119 us (42%)
  Pallas kernels  78.7 us (28%)
  starting transfers between devices  39 us (14%)
  local copies, waits for them, and re-layouts  27.8 us (10%)
  other arithmetic  17.8 us (6%)
    pallas_call x4, Pallas kernels, attend(): pl.pallas_call(kernel, grid_spec=grid_spec, out_shape=[jax.ShapeDtypeStru...  78.7 us
    all_to_all x2, waiting for transfers between devices, exchange_out(): lax.all_to_all(split, 'head', split_axis=0, concat_axis=0, tiled=True)  59.6 us
    all_to_all x2, waiting for transfers between devices, exchange_in(): lax.all_to_all(stacked, 'head', split_axis=0, concat_axis=0, tiled=True)  59.2 us
    ppermute x4, starting transfers between devices, shifted(): return lax.ppermute(block, axis, route)  13.7 us
    all_to_all x2, starting transfers between devices, exchange_out(): lax.all_to_all(split, 'head', split_axis=0, concat_axis=0, tiled=True)  13.5 us
    all_to_all x2, starting transfers between devices, exchange_in(): lax.all_to_all(stacked, 'head', split_axis=0, concat_axis=0, tiled=True)  11.9 us
    concatenate x1, other arithmetic, body(): jnp.concatenate([second_out, key_grad, value_grad], axis=1)  8.83 us
    unnamed x23, local copies, waits for them, and re-layouts  8.35 us
  transfers between devices with their start and end apart: 8, of which 3 were waited for; matrix products, arithmetic and copies ran while one was open for 10% of the time, Pallas kernels for 28%

profile of v3, /device:TPU:121, one launch (start us, length us, event | category | flops | bytes accessed | tf_op | source)
XLA Modules:
  0.0 283.4 jit_solution(557306441694831367)
XLA Ops:
  0.6 2.3 copy.37
  7.0 2.3 maximum_bitcast_fusion
  9.3 5.9 %all-to-all-start = ((bf16[16,256,512]{2,1,0:T(8,128)(2,1)}), bf16[16,256,512]{2,1,0:T(8,128)(2,1)}, u32[]{:S(2)}, u32[]{:S(2)}) async-start(bf16[16,256,512]{2,1,0:T(8,128)(2,1)} %maximum_bitcast_fusion), calls=%async_computation | async-start | bytes 8388608 | tf_op jit(solution)/shard_map/all_to_all | solution.py:129
  15.8 1.6 maximum_bitcast_fusion.1
  17.4 59.2 %all-to-all-done = bf16[16,256,512]{2,1,0:T(8,128)(2,1)} async-done(((bf16[16,256,512]{2,1,0:T(8,128)(2,1)}), bf16[16,256,512]{2,1,0:T(8,128)(2,1)}, u32[]{:S(2)}, u32[]{:S(2)}) %all-to-all-start) | async-done | bytes 4194336 | tf_op jit(solution)/shard_map/all_to_all | solution.py:129
  76.6 5.9 %all-to-all-start.2 = ((bf16[16,256,256]{2,1,0:T(8,128)(2,1)}), bf16[16,256,256]{2,1,0:T(8,128)(2,1)S(1)}, u32[]{:S(2)}, u32[]{:S(2)}) async-start(bf16[16,256,256]{2,1,0:T(8,128)(2,1)} %maximum_bitcast_fusion.1), calls=%async_computation.2 | async-start | bytes 4194304 | tf_op jit(solution)/shard_map/all_to_all | solution.py:129
  83.6 4.4 %collective-permute-start.1 = (bf16[1024,128]{1,0:T(8,128)(2,1)S(1)}, bf16[1024,128]{1,0:T(8,128)(2,1)S(1)}, u32[]{:S(2)}, u32[]{:S(2)}) collective-permute-start(bf16[1024,128]{1,0:T(8,128)(2,1)S(1)} %get-tuple-element.32), channel_id=1, source_target_pairs={{0,16},{16,32},{32,48},{48,64},{64,80},{80,96},{96,112},{1,17},{17... | collective-permute-start | bytes 786440 | tf_op jit(solution)/shard_map/ppermute | solution.py:21
  88.0 3.0 %fusion.1 = (bf16[4096,128]{1,0:T(8,128)(2,1)}, bf16[4096,128]{1,0:T(8,128)(2,1)}) fusion(bf16[4096,512]{1,0:T(8,128)(2,1)} %bitcast.2.q_ref.g_ref), kind=kLoop, calls=%fused_computation.20 | loop fusion | bytes 4194304 | tf_op jit(solution)/shard_map/slice | solution.py:157
  91.0 1.9 collective-permute-start
  92.9 25.4 %shard_map.75 = (bf16[4096,256]{1,0:T(8,128)(2,1)}, f32[5120,128]{1,0:T(8,128)}, f32[5120,128]{1,0:T(8,128)}) custom-call(s32[1]{0:T(128)} %bitcast.first_ref, bf16[4096,512]{1,0:T(8,128)(2,1)} %bitcast.2.q_ref.g_ref, bf16[4096,512]{1,0:T(8,128)(2,1)} %bitcast.2.q_ref.g_ref, bf16[4096,128]{1,0:T(8,128)(2,1)} %get-tuple-element.35.k_ref, ...), custom_call_target="tpu_custom_call" | custom-call | tf_op jit(solution)/shard_map/pallas_call | solution.py:112
  118.3 1.2 pad_maximum_fusion.1.v_ref
  120.0 1.1 pad_maximum_fusion.k_ref
  121.2 13.0 %shard_map.76 = (bf16[4096,256]{1,0:T(8,128)(2,1)}, f32[5120,128]{1,0:T(8,128)}, f32[5120,128]{1,0:T(8,128)}) custom-call(s32[1]{0:T(128)} %bitcast.first_ref, bf16[4096,512]{1,0:T(8,128)(2,1)} %bitcast.2.q_ref.g_ref, bf16[4096,512]{1,0:T(8,128)(2,1)} %bitcast.2.q_ref.g_ref, ...), custom_call_target="tpu_custom_call", output_to_operand_aliasing={{0}: (5, {}), {1}: (6, {}), {2}: (7, {})} | custom-call | tf_op jit(solution)/shard_map/pallas_call | solution.py:112
  134.2 7.1 %all-to-all-start.1 = ((bf16[16,256,256]{2,1,0:T(8,128)(2,1)}), bf16[16,256,256]{2,1,0:T(8,128)(2,1)}, u32[]{:S(2)}, u32[]{:S(2)}) async-start(bf16[16,256,256]{2,1,0:T(8,128)(2,1)} %bitcast.48), calls=%async_computation.1 | async-start | bytes 4194304 | tf_op jit(solution)/shard_map/all_to_all | solution.py:136
  141.3 1.5 broadcast_in_dim.3.rest_0_
  142.8 13.1 %shard_map.77 = (bf16[4096,256]{1,0:T(8,128)(2,1)}, f32[5120,128]{1,0:T(8,128)}, f32[5120,128]{1,0:T(8,128)}) custom-call(s32[1]{0:T(128)} %bitcast.first_ref, bf16[4096,256]{1,0:T(8,128)(2,1)} %bitcast.41, bf16[4096,256]{1,0:T(8,128)(2,1)} %bitcast.42, ...), custom_call_target="tpu_custom_call", output_to_operand_aliasing={{0}: (5, {}), {1}: (6, {}), {2}: (7, {})} | custom-call | tf_op jit(solution)/shard_map/pallas_call | solution.py:112
  157.0 4.8 %collective-permute-start.2 = (bf16[1024,128]{1,0:T(8,128)(2,1)S(1)}, bf16[1024,128]{1,0:T(8,128)(2,1)S(1)}, u32[]{:S(2)}, u32[]{:S(2)}) collective-permute-start(bf16[1024,128]{1,0:T(8,128)(2,1)S(1)} %slice.115), channel_id=1, source_target_pairs={{16,0},{32,16},{48,32},{64,48},{80,64},{96,80},{112,96},{17,1},{33... | collective-permute-start | bytes 786440 | tf_op jit(solution)/shard_map/ppermute | solution.py:21
  162.9 2.6 collective-permute-start.3
  165.5 27.1 %shard_map.78 = (bf16[4096,256]{1,0:T(8,128)(2,1)}, f32[5120,128]{1,0:T(8,128)}, f32[5120,128]{1,0:T(8,128)}) custom-call(s32[1]{0:T(128)} %bitcast.first_ref, bf16[4096,256]{1,0:T(8,128)(2,1)} %bitcast.43, bf16[4096,256]{1,0:T(8,128)(2,1)} %bitcast.44, ...), custom_call_target="tpu_custom_call", output_to_operand_aliasing={{0}: (5, {}), {1}: (6, {}), {2}: (7, {})} | custom-call | tf_op jit(solution)/shard_map/pallas_call | solution.py:112
  192.6 1.6 slice.112
  194.2 1.5 slice.113
  195.7 1.1 add_convert_fusion.1
  196.8 1.1 add_convert_fusion
  197.9 8.8 %maximum_maximum_fusion = bf16[4096,512]{1,0:T(8,128)(2,1)} fusion(bf16[1024,128]{1,0:T(8,128)(2,1)S(1)} %add_convert_fusion, bf16[3072,128]{1,0:T(8,128)(2,1)S(1)} %slice.112, bf16[1024,128]{1,0:T(8,128)(2,1)S(1)} %add_convert_fusion.1, bf16[3072,128]{1,0:T(8,128)(2,1)S(1)} %slice.113, bf16[4096,256]{1,0:T(8,128)(2,1)S(1)} %copy-done.3), kind=kLoop, calls=%fused_computation.1 | loop fusion | flops 20971520 | bytes 8388608 | tf_op jit(solution)/shard_map/concatenate | solution.py:187
  206.8 6.3 %all-to-all-start.3 = ((bf16[16,256,512]{2,1,0:T(8,128)(2,1)}), bf16[16,256,512]{2,1,0:T(8,128)(2,1)}, u32[]{:S(2)}, u32[]{:S(2)}) async-start(bf16[16,256,512]{2,1,0:T(8,128)(2,1)} %bitcast.45), calls=%async_computation.3 | async-start | bytes 8388608 | tf_op jit(solution)/shard_map/all_to_all | solution.py:136
  213.1 1.7 fusion.2
  214.8 59.6 %all-to-all-done.3 = bf16[16,256,512]{2,1,0:T(8,128)(2,1)} async-done(((bf16[16,256,512]{2,1,0:T(8,128)(2,1)}), bf16[16,256,512]{2,1,0:T(8,128)(2,1)}, u32[]{:S(2)}, u32[]{:S(2)}) %all-to-all-start.3) | async-done | bytes 4194336 | tf_op jit(solution)/shard_map/all_to_all | solution.py:136
  274.4 2.7 slice_bitcast_fusion
  277.5 1.6 copy.34
  279.3 1.6 copy.33
  280.9 1.3 copy.43
  282.2 1.3 copy.44
  (35 shorter events, 8.8 us)
Async XLA Ops:
  0.6 5.2 %copy-start = (bf16[256,2048]{1,0:T(8,128)(2,1)S(1)}, bf16[256,2048]{1,0:T(8,128)(2,1)}, u32[]{:S(2)}) copy-start(bf16[256,2048]{1,0:T(8,128)(2,1)} %param.5) | copy-start | bytes 3145732
  3.0 1.6 copy-start.6
  5.2 1.2 copy-start.7
  9.3 67.3 %all-to-all-start = ((bf16[16,256,512]{2,1,0:T(8,128)(2,1)}), bf16[16,256,512]{2,1,0:T(8,128)(2,1)}, u32[]{:S(2)}, u32[]{:S(2)}) async-start(bf16[16,256,512]{2,1,0:T(8,128)(2,1)} %maximum_bitcast_fusion), calls=%async_computation | async-start | bytes 8388608 | tf_op jit(solution)/shard_map/all_to_all | solution.py:129
  76.6 57.6 %all-to-all-start.2 = ((bf16[16,256,256]{2,1,0:T(8,128)(2,1)}), bf16[16,256,256]{2,1,0:T(8,128)(2,1)S(1)}, u32[]{:S(2)}, u32[]{:S(2)}) async-start(bf16[16,256,256]{2,1,0:T(8,128)(2,1)} %maximum_bitcast_fusion.1), calls=%async_computation.2 | async-start | bytes 4194304 | tf_op jit(solution)/shard_map/all_to_all | solution.py:129
  83.6 34.7 %collective-permute-start.1 = (bf16[1024,128]{1,0:T(8,128)(2,1)S(1)}, bf16[1024,128]{1,0:T(8,128)(2,1)S(1)}, u32[]{:S(2)}, u32[]{:S(2)}) collective-permute-start(bf16[1024,128]{1,0:T(8,128)(2,1)S(1)} %get-tuple-element.32), channel_id=1, source_target_pairs={{0,16},{16,32},{32,48},{48,64},{64,80},{80,96},{96,112},{1,17},{17... | collective-permute-start | bytes 786440 | tf_op jit(solution)/shard_map/ppermute | solution.py:21
  91.0 29.0 %collective-permute-start = (bf16[1024,128]{1,0:T(8,128)(2,1)S(1)}, bf16[1024,128]{1,0:T(8,128)(2,1)S(1)}, u32[]{:S(2)}, u32[]{:S(2)}) collective-permute-start(bf16[1024,128]{1,0:T(8,128)(2,1)S(1)} %get-tuple-element.33), channel_id=1, source_target_pairs={{0,16},{16,32},{32,48},{48,64},{64,80},{80,96},{96,112},{1,17},{17... | collective-permute-start | bytes 786440 | tf_op jit(solution)/shard_map/ppermute | solution.py:21
  92.9 25.5 %copy-start.5 = (bf16[4096,128]{1,0:T(8,128)(2,1)S(1)}, bf16[4096,128]{1,0:T(8,128)(2,1)}, u32[]{:S(2)}) copy-start(bf16[4096,128]{1,0:T(8,128)(2,1)} %get-tuple-element.34.v_ref) | copy-start | bytes 3145732
  118.3 1.7 copy-start.4
  134.2 8.6 %copy-start.2 = (bf16[16,256,256]{2,1,0:T(8,128)(2,1)}, bf16[16,256,256]{2,1,0:T(8,128)(2,1)S(1)}, u32[]{:S(2)}) copy-start(bf16[16,256,256]{2,1,0:T(8,128)(2,1)S(1)} %all-to-all-done.2) | copy-start | bytes 6291460
  134.2 72.6 %all-to-all-start.1 = ((bf16[16,256,256]{2,1,0:T(8,128)(2,1)}), bf16[16,256,256]{2,1,0:T(8,128)(2,1)}, u32[]{:S(2)}, u32[]{:S(2)}) async-start(bf16[16,256,256]{2,1,0:T(8,128)(2,1)} %bitcast.48), calls=%async_computation.1 | async-start | bytes 4194304 | tf_op jit(solution)/shard_map/all_to_all | solution.py:136
  157.0 38.8 %collective-permute-start.2 = (bf16[1024,128]{1,0:T(8,128)(2,1)S(1)}, bf16[1024,128]{1,0:T(8,128)(2,1)S(1)}, u32[]{:S(2)}, u32[]{:S(2)}) collective-permute-start(bf16[1024,128]{1,0:T(8,128)(2,1)S(1)} %slice.115), channel_id=1, source_target_pairs={{16,0},{32,16},{48,32},{64,48},{80,64},{96,80},{112,96},{17,1},{33... | collective-permute-start | bytes 786440 | tf_op jit(solution)/shard_map/ppermute | solution.py:21
  162.9 33.9 %collective-permute-start.3 = (bf16[1024,128]{1,0:T(8,128)(2,1)S(1)}, bf16[1024,128]{1,0:T(8,128)(2,1)S(1)}, u32[]{:S(2)}, u32[]{:S(2)}) collective-permute-start(bf16[1024,128]{1,0:T(8,128)(2,1)S(1)} %slice.114), channel_id=1, source_target_pairs={{16,0},{32,16},{48,32},{64,48},{80,64},{96,80},{112,96},{17,1},{33... | collective-permute-start | bytes 786440 | tf_op jit(solution)/shard_map/ppermute | solution.py:21
  192.6 5.4 %copy-start.3 = (bf16[4096,256]{1,0:T(8,128)(2,1)S(1)}, bf16[4096,256]{1,0:T(8,128)(2,1)}, u32[]{:S(2)}) copy-start(bf16[4096,256]{1,0:T(8,128)(2,1)} %get-tuple-element.25) | copy-start | bytes 6291460
  206.8 67.7 %all-to-all-start.3 = ((bf16[16,256,512]{2,1,0:T(8,128)(2,1)}), bf16[16,256,512]{2,1,0:T(8,128)(2,1)}, u32[]{:S(2)}, u32[]{:S(2)}) async-start(bf16[16,256,512]{2,1,0:T(8,128)(2,1)} %bitcast.45), calls=%async_computation.3 | async-start | bytes 8388608 | tf_op jit(solution)/shard_map/all_to_all | solution.py:136
  279.3 4.1 %copy-start.1 = (bf16[256,2048]{1,0:T(8,128)(2,1)S(1)}, bf16[256,2048]{1,0:T(8,128)(2,1)}, u32[]{:S(2)}) copy-start(bf16[256,2048]{1,0:T(8,128)(2,1)} %param.5) | copy-start | bytes 3145732

commit v4 on v3

v4 whole, which is shorter than its diff:
```python
import functools

import jax
import jax.numpy as jnp
from jax import lax
from jax.experimental import pallas as pl
from jax.experimental.pallas import tpu as pltpu
from jax.sharding import PartitionSpec as P

HD = 128
QH = 32
KVH = 16
WIN = 1024
QPRE = 168
BLK = 256


def shifted(block, axis, distance):
    devices = range(lax.axis_size(axis))
    route = [(i - distance, i) for i in devices if i - distance in devices]
    return lax.ppermute(block, axis, route)


def attend_kernel(first_ref, *refs, heads, block_offset, key_shift, carry):
    q_refs = refs[0 : 2 * heads : 2]
    g_refs = refs[1 : 2 * heads : 2]
    k_ref, v_ref = refs[2 * heads : 2 * heads + 2]
    rest = refs[2 * heads + 2 :]
    if carry:
        rest = rest[heads:]
        dk_in_ref, dv_in_ref = rest[:2]
        rest = rest[2:]
    od_refs = rest[:heads]
    dk_ref, dv_ref = rest[heads:]
    step = pl.program_id(0)
    block = step + block_offset
    rows = q_refs[0].shape[0]
    span = WIN + rows
    scale = QPRE ** (-0.5)

    @pl.when(step == 0)
    def _():
        if carry:
            dk_ref[...] = dk_in_ref[...]
            dv_ref[...] = dv_in_ref[...]
        else:
            dk_ref[...] = jnp.zeros_like(dk_ref)
            dv_ref[...] = jnp.zeros_like(dv_ref)

    start = pl.multiple_of(block * rows, rows)
    key_start = pl.multiple_of(block * rows - key_shift, rows)
    k_win = k_ref[pl.ds(key_start, span), :]
    v_win = v_ref[pl.ds(key_start, span), :]
    row_id = lax.broadcasted_iota(jnp.int32, (rows, span), 0)
    col_id = lax.broadcasted_iota(jnp.int32, (rows, span), 1)
    distance = row_id + WIN - col_id
    key_pos = first_ref[0] - WIN + start + col_id
    allowed = (distance >= 0) & (distance < WIN) & (key_pos >= 0)
    nt = (((1,), (1,)), ((), ()))
    tn = (((0,), (0,)), ((), ()))
    dk_acc = None
    dv_acc = None
    for q_ref, g_ref, od_ref in zip(q_refs, g_refs, od_refs):
        q = q_ref[...]
        g = g_ref[...]
        scores = lax.dot_general(q, k_win, nt, preferred_element_type=jnp.float32) * scale
        scores = jnp.where(allowed, scores, -jnp.inf)
        largest = jnp.max(scores, axis=-1, keepdims=True)
        unnormed = jnp.exp(scores - largest)
        probs = unnormed * (1.0 / jnp.sum(unnormed, axis=-1, keepdims=True))
        probs_low = probs.astype(jnp.bfloat16)
        out = jnp.dot(probs_low, v_win, preferred_element_type=jnp.float32).astype(jnp.bfloat16)
        od_ref[:, :HD] = out
        grad_probs = lax.dot_general(g, v_win, nt, preferred_element_type=jnp.float32)
        inner = jnp.sum(g.astype(jnp.float32) * out.astype(jnp.float32), axis=-1, keepdims=True)
        grad_scores = (probs * (grad_probs - inner) * scale).astype(jnp.bfloat16)
        od_ref[:, HD:] = jnp.dot(grad_scores, k_win, preferred_element_type=jnp.float32).astype(
            jnp.bfloat16
        )
        dk_part = lax.dot_general(grad_scores, q, tn, preferred_element_type=jnp.float32)
        dv_part = lax.dot_general(probs_low, g, tn, preferred_element_type=jnp.float32)
        dk_acc = dk_part if dk_acc is None else dk_acc + dk_part
        dv_acc = dv_part if dv_acc is None else dv_acc + dv_part
    dk_ref[pl.ds(start, span), :] += dk_acc
    dv_ref[pl.ds(start, span), :] += dv_acc


def attend(sources, keys, values, first_query, blocks, key_shift, carried=None):
    heads = len(sources)
    query_count = sources[0][0].shape[0]
    ext_rows = WIN + query_count
    rows = BLK
    block_offset, block_count = blocks
    first = jnp.reshape(first_query, (1,)).astype(jnp.int32)
    key_spec = pl.BlockSpec(keys.shape, lambda b, f: (0, 0))
    whole = pl.BlockSpec((ext_rows, HD), lambda b, f: (0, 0))
    in_specs = []
    operands = [first]
    for source, q_col, g_col in sources:
        in_specs += [
            pl.BlockSpec((rows, HD), lambda b, f, c=q_col: (b + block_offset, c)),
            pl.BlockSpec((rows, HD), lambda b, f, c=g_col: (b + block_offset, c)),
        ]
        operands += [source, source]
    in_specs += [key_spec, key_spec]
    operands += [keys, values]
    aliases = {}
    if carried is not None:
        base = len(operands)
        in_specs += [pl.BlockSpec(memory_space=pl.ANY)] * heads + [whole, whole]
        operands += list(carried)
        aliases = {base + i: i for i in range(heads + 2)}
    grid_spec = pltpu.PrefetchScalarGridSpec(
        num_scalar_prefetch=1,
        grid=(block_count,),
        in_specs=in_specs,
        out_specs=[pl.BlockSpec((rows, 2 * HD), lambda b, f: (b + block_offset, 0))] * heads
        + [whole, whole],
    )
    kernel = functools.partial(
        attend_kernel,
        heads=heads,
        block_offset=block_offset,
        key_shift=key_shift,
        carry=carried is not None,
    )
    return pl.pallas_call(
        kernel,
        grid_spec=grid_spec,
        out_shape=[jax.ShapeDtypeStruct((query_count, 2 * HD), jnp.bfloat16)] * heads
        + [
            jax.ShapeDtypeStruct((ext_rows, HD), jnp.float32),
            jax.ShapeDtypeStruct((ext_rows, HD), jnp.float32),
        ],
        input_output_aliases=aliases,
        compiler_params=pltpu.CompilerParams(
            dimension_semantics=("arbitrary",), vmem_limit_bytes=56 * 1024 * 1024
        ),
    )(*operands)


def exchange_in(pieces):
    stacked = jnp.transpose(jnp.concatenate(pieces, axis=-1), (1, 0, 2))
    moved = lax.all_to_all(stacked, "head", split_axis=0, concat_axis=0, tiled=True)
    return moved.reshape(moved.shape[0] * moved.shape[1], moved.shape[2])


def exchange_out(group_block):
    shared = lax.axis_size("head")
    split = group_block.reshape(shared, group_block.shape[0] // shared, group_block.shape[1])
    moved = lax.all_to_all(split, "head", split_axis=0, concat_axis=0, tiled=True)
    return jnp.transpose(moved, (1, 0, 2))


def body(queries, keys, values, grad_out):
    token_count = queries.shape[0]
    shared = KVH
    pair = (QH // KVH) * HD
    query_rows = queries.reshape(token_count, shared, pair)
    grad_rows = grad_out.reshape(token_count, shared, pair)
    key_rows = keys.reshape(token_count, shared, HD)
    value_rows = values.reshape(token_count, shared, HD)
    first_part = exchange_in(
        [key_rows, value_rows, query_rows[:, :, :HD], grad_rows[:, :, :HD]]
    )
    second_part = exchange_in([query_rows[:, :, HD:], grad_rows[:, :, HD:]])
    group_rows = first_part.shape[0]
    block_total = group_rows // BLK
    lead = WIN // BLK
    first_query = lax.axis_index("ctx") * group_rows
    group_keys = first_part[:, :HD]
    group_values = first_part[:, HD : 2 * HD]
    tail = shifted(first_part[group_rows - WIN :, : 2 * HD], "ctx", 1)
    late = (lead, block_total - lead)
    early = (0, lead)
    head0 = (first_part, 2, 3)
    head1 = (second_part, 0, 1)
    carried = attend([head0], group_keys, group_values, first_query, late, WIN)
    keys_ext = jnp.concatenate([tail[:, :HD], group_keys], axis=0)
    values_ext = jnp.concatenate([tail[:, HD:], group_values], axis=0)
    first_out, second_out, key_acc, value_acc = attend(
        [head0, head1], keys_ext, values_ext, first_query, early, 0,
        (carried[0], jnp.zeros_like(carried[0]), carried[1], carried[2]),
    )
    back = shifted(
        jnp.concatenate([key_acc[:WIN], value_acc[:WIN]], axis=1).astype(jnp.bfloat16), "ctx", -1
    ).astype(jnp.float32)
    second_out, key_total, value_total = attend(
        [head1], keys_ext, values_ext, first_query, late, 0, (second_out, key_acc, value_acc)
    )
    key_grad = jnp.concatenate(
        [key_total[WIN:group_rows], key_total[group_rows:] + back[:, :HD]], axis=0
    ).astype(jnp.bfloat16)
    value_grad = jnp.concatenate(
        [value_total[WIN:group_rows], value_total[group_rows:] + back[:, HD:]], axis=0
    ).astype(jnp.bfloat16)
    first_back = exchange_out(first_out)
    second_back = exchange_out(jnp.concatenate([second_out, key_grad, value_grad], axis=1))
    attended = jnp.concatenate([first_back[:, :, :HD], second_back[:, :, :HD]], axis=2)
    grad_queries = jnp.concatenate(
        [first_back[:, :, HD:], second_back[:, :, HD : 2 * HD]], axis=2
    )
    return (
        attended.reshape(token_count, QH * HD),
        grad_queries.reshape(token_count, QH * HD),
        second_back[:, :, 2 * HD : 3 * HD].reshape(token_count, KVH * HD),
        second_back[:, :, 3 * HD :].reshape(token_count, KVH * HD),
    )


def solution(mesh):
    placed = (
        P(("ctx", "head"), None),
        P(("ctx", "head"), None),
        P(("ctx", "head"), None),
        P(("ctx", "head"), None),
    )
    return jax.shard_map(
        body,
        mesh=mesh,
        in_specs=placed,
        out_specs=(
            P(("ctx", "head"), None),
            P(("ctx", "head"), None),
            P(("ctx", "head"), None),
            P(("ctx", "head"), None),
        ),
        check_vma=False,
    )
```

time: 285 us -> 278 us (0.975)
  Pallas kernels: 78.7 us -> 71.8 us
  starting transfers between devices: 39 us -> 34.3 us
  waiting for transfers between devices: 119 us -> 123 us
    pallas_call x4 -> x3, Pallas kernels: 78.7 us -> 71.8 us  [attend(): pl.pallas_call(kernel, grid_spec=grid_spec, out_shape=[jax.ShapeDtypeStru...]
    ppermute x4 -> x2, starting transfers between devices: 13.7 us -> 8.03 us  [shifted(): return lax.ppermute(block, axis, route)]
    ppermute x4 -> x2, waiting for transfers between devices: 0.43 us -> 4.3 us  [shifted(): return lax.ppermute(block, axis, route)]
    unnamed x23 -> x25, local copies, waits for them, and re-layouts: 8.35 us -> 8.74 us
  transfers between devices with their start and end apart: 8 -> 6, of which waited for: 3 -> 4; matrix products, arithmetic and copies ran while one was open for 10% -> 9% of each run, Pallas kernels for 28% -> 19%
where the time goes in v4:
time: 278 us; the launch traced here: 276 us
  waiting for transfers between devices  123 us (44%)
  Pallas kernels  71.8 us (26%)
  starting transfers between devices  34.3 us (12%)
  local copies, waits for them, and re-layouts  28.2 us (10%)
  other arithmetic  17.2 us (6%)
    pallas_call x3, Pallas kernels, attend(): pl.pallas_call(kernel, grid_spec=grid_spec, out_shape=[jax.ShapeDtypeStru...  71.8 us
    all_to_all x2, waiting for transfers between devices, exchange_out(): lax.all_to_all(split, 'head', split_axis=0, concat_axis=0, tiled=True)  59.8 us
    all_to_all x2, waiting for transfers between devices, exchange_in(): lax.all_to_all(stacked, 'head', split_axis=0, concat_axis=0, tiled=True)  59.2 us
    all_to_all x2, starting transfers between devices, exchange_out(): lax.all_to_all(split, 'head', split_axis=0, concat_axis=0, tiled=True)  14.5 us
    all_to_all x2, starting transfers between devices, exchange_in(): lax.all_to_all(stacked, 'head', split_axis=0, concat_axis=0, tiled=True)  11.9 us
    concatenate x1, other arithmetic, body(): jnp.concatenate([second_out, key_grad, value_grad], axis=1)  8.93 us
    unnamed x25, local copies, waits for them, and re-layouts  8.74 us
    ppermute x2, starting transfers between devices, shifted(): return lax.ppermute(block, axis, route)  8.03 us
  transfers between devices with their start and end apart: 6, of which 4 were waited for; matrix products, arithmetic and copies ran while one was open for 9% of the time, Pallas kernels for 19%

profile of v4, /device:TPU:121, one launch (start us, length us, event | category | flops | bytes accessed | tf_op | source)
XLA Modules:
  0.0 275.7 jit_solution(16718695328180117133)
XLA Ops:
  0.6 2.3 copy.35
  7.0 2.3 maximum_bitcast_fusion
  9.3 5.9 %all-to-all-start = ((bf16[16,256,512]{2,1,0:T(8,128)(2,1)}), bf16[16,256,512]{2,1,0:T(8,128)(2,1)}, u32[]{:S(2)}, u32[]{:S(2)}) async-start(bf16[16,256,512]{2,1,0:T(8,128)(2,1)} %maximum_bitcast_fusion), calls=%async_computation | async-start | bytes 8388608 | tf_op jit(solution)/shard_map/all_to_all | solution.py:144
  15.8 1.6 maximum_bitcast_fusion.1
  17.4 59.2 %all-to-all-done = bf16[16,256,512]{2,1,0:T(8,128)(2,1)} async-done(((bf16[16,256,512]{2,1,0:T(8,128)(2,1)}), bf16[16,256,512]{2,1,0:T(8,128)(2,1)}, u32[]{:S(2)}, u32[]{:S(2)}) %all-to-all-start) | async-done | bytes 4194336 | tf_op jit(solution)/shard_map/all_to_all | solution.py:144
  76.6 5.9 %all-to-all-start.1 = ((bf16[16,256,256]{2,1,0:T(8,128)(2,1)}), bf16[16,256,256]{2,1,0:T(8,128)(2,1)S(1)}, u32[]{:S(2)}, u32[]{:S(2)}) async-start(bf16[16,256,256]{2,1,0:T(8,128)(2,1)} %maximum_bitcast_fusion.1), calls=%async_computation.1 | async-start | bytes 4194304 | tf_op jit(solution)/shard_map/all_to_all | solution.py:144
  82.5 1.1 slice.100
  83.6 4.4 %collective-permute-start = (bf16[1024,256]{1,0:T(8,128)(2,1)S(1)}, bf16[1024,256]{1,0:T(8,128)(2,1)S(1)}, u32[]{:S(2)}, u32[]{:S(2)}) collective-permute-start(bf16[1024,256]{1,0:T(8,128)(2,1)S(1)} %slice.100), channel_id=1, source_target_pairs={{0,16},{16,32},{32,48},{48,64},{64,80},{80,96},{96,112},{1,17},{17... | collective-permute-start | bytes 1572872 | tf_op jit(solution)/shard_map/ppermute | solution.py:21
  88.0 3.0 %fusion.2 = (bf16[4096,128]{1,0:T(8,128)(2,1)}, bf16[4096,128]{1,0:T(8,128)(2,1)}) fusion(bf16[4096,512]{1,0:T(8,128)(2,1)} %bitcast.2.refs_0_.refs_1_), kind=kLoop, calls=%fused_computation.22 | loop fusion | bytes 4194304 | tf_op jit(solution)/shard_map/slice | solution.py:172
  91.0 25.4 %shard_map.75 = (bf16[4096,256]{1,0:T(8,128)(2,1)}, f32[5120,128]{1,0:T(8,128)}, f32[5120,128]{1,0:T(8,128)}) custom-call(s32[1]{0:T(128)} %bitcast.first_ref, bf16[4096,512]{1,0:T(8,128)(2,1)} %bitcast.2.refs_0_.refs_1_, bf16[4096,512]{1,0:T(8,128)(2,1)} %bitcast.2.refs_0_.refs_1_, bf16[4096,128]{1,0:T(8,128)(2,1)} %get-tuple-element.29.refs_2_, ...), custom_call_target="tpu_custom_call" | custom-call | tf_op jit(solution)/shard_map/pallas_call | solution.py:127
  116.4 3.6 %collective-permute-done = bf16[1024,256]{1,0:T(8,128)(2,1)S(1)} collective-permute-done((bf16[1024,256]{1,0:T(8,128)(2,1)S(1)}, bf16[1024,256]{1,0:T(8,128)(2,1)S(1)}, u32[]{:S(2)}, u32[]{:S(2)}) %collective-permute-start) | collective-permute-done | bytes 524320 | tf_op jit(solution)/shard_map/ppermute | solution.py:21
  120.0 1.1 pad_maximum_fusion.1.refs_5_.refs_3_
  121.2 1.2 pad_maximum_fusion.refs_4_.refs_2_
  122.4 1.6 broadcast_in_dim.3.refs_7_
  124.4 19.2 %shard_map.76 = (bf16[4096,256]{1,0:T(8,128)(2,1)}, bf16[4096,256]{1,0:T(8,128)(2,1)}, f32[5120,128]{1,0:T(8,128)}, f32[5120,128]{1,0:T(8,128)}) custom-call(s32[1]{0:T(128)} %bitcast.first_ref, bf16[4096,512]{1,0:T(8,128)(2,1)} %bitcast.2.refs_0_.refs_1_, ...), custom_call_target="tpu_custom_call", output_to_operand_aliasing={{0}: (7, {}), {1}: (8, {}), {2}: (9, {}), {3}: (10, {})} | custom-call | tf_op jit(solution)/shard_map/pallas_call | solution.py:127
  143.6 7.2 %all-to-all-start.2 = ((bf16[16,256,256]{2,1,0:T(8,128)(2,1)}), bf16[16,256,256]{2,1,0:T(8,128)(2,1)S(1)}, u32[]{:S(2)}, u32[]{:S(2)}) async-start(bf16[16,256,256]{2,1,0:T(8,128)(2,1)} %bitcast.49), calls=%async_computation.2 | async-start | bytes 4194304 | tf_op jit(solution)/shard_map/all_to_all | solution.py:151
  150.9 1.1 slice.134
  151.9 1.1 slice.133
  153.1 3.7 %collective-permute-start.1 = (bf16[1024,256]{1,0:T(8,128)(2,1)S(1)}, bf16[1024,256]{1,0:T(8,128)(2,1)S(1)}, u32[]{:S(2)}, u32[]{:S(2)}) collective-permute-start(bf16[1024,256]{1,0:T(8,128)(2,1)S(1)} %pad_maximum_fusion.2), channel_id=1, source_target_pairs={{16,0},{32,16},{48,32},{64,48},{80,64},{96,80},{112,96},{17,1},{33... | collective-permute-start | bytes 1572872 | tf_op jit(solution)/shard_map/ppermute | solution.py:21
  156.8 27.1 %shard_map.77 = (bf16[4096,256]{1,0:T(8,128)(2,1)}, f32[5120,128]{1,0:T(8,128)}, f32[5120,128]{1,0:T(8,128)}) custom-call(s32[1]{0:T(128)} %bitcast.first_ref, bf16[4096,256]{1,0:T(8,128)(2,1)} %bitcast.43, bf16[4096,256]{1,0:T(8,128)(2,1)} %bitcast.44, ...), custom_call_target="tpu_custom_call", output_to_operand_aliasing={{0}: (5, {}), {1}: (6, {}), {2}: (7, {})} | custom-call | tf_op jit(solution)/shard_map/pallas_call | solution.py:127
  183.9 1.5 slice.131
  185.4 1.6 slice.132
  187.9 1.3 fusion.1
  189.2 8.9 %maximum_maximum_fusion = bf16[4096,512]{1,0:T(8,128)(2,1)} fusion(bf16[1024,128]{1,0:T(8,128)(2,1)S(1)} %get-tuple-element.37, bf16[3072,128]{1,0:T(8,128)(2,1)S(1)} %slice.131, bf16[1024,128]{1,0:T(8,128)(2,1)S(1)} %get-tuple-element.36, bf16[3072,128]{1,0:T(8,128)(2,1)S(1)} %slice.132, bf16[4096,256]{1,0:T(8,128)(2,1)S(1)} %copy-done.3), kind=kLoop, calls=%fused_computation.1 | loop fusion | flops 20971520 | bytes 8388608 | tf_op jit(solution)/shard_map/concatenate | solution.py:198
  198.1 7.2 %all-to-all-start.3 = ((bf16[16,256,512]{2,1,0:T(8,128)(2,1)}), bf16[16,256,512]{2,1,0:T(8,128)(2,1)}, u32[]{:S(2)}, u32[]{:S(2)}) async-start(bf16[16,256,512]{2,1,0:T(8,128)(2,1)} %bitcast.45), calls=%async_computation.3 | async-start | bytes 8388608 | tf_op jit(solution)/shard_map/all_to_all | solution.py:151
  205.3 1.5 fusion.3
  206.9 59.8 %all-to-all-done.3 = bf16[16,256,512]{2,1,0:T(8,128)(2,1)} async-done(((bf16[16,256,512]{2,1,0:T(8,128)(2,1)}), bf16[16,256,512]{2,1,0:T(8,128)(2,1)}, u32[]{:S(2)}, u32[]{:S(2)}) %all-to-all-start.3) | async-done | bytes 4194336 | tf_op jit(solution)/shard_map/all_to_all | solution.py:151
  266.7 2.7 slice_bitcast_fusion
  269.4 1.3 copy.41
  270.6 1.3 copy.42
  272.2 1.6 copy.32
  274.1 1.6 copy.31
  (34 shorter events, 6.5 us)
Async XLA Ops:
  0.6 5.2 %copy-start = (bf16[256,2048]{1,0:T(8,128)(2,1)S(1)}, bf16[256,2048]{1,0:T(8,128)(2,1)}, u32[]{:S(2)}) copy-start(bf16[256,2048]{1,0:T(8,128)(2,1)} %param.5) | copy-start | bytes 3145732
  3.0 1.6 copy-start.7
  5.2 1.2 copy-start.8
  9.3 67.3 %all-to-all-start = ((bf16[16,256,512]{2,1,0:T(8,128)(2,1)}), bf16[16,256,512]{2,1,0:T(8,128)(2,1)}, u32[]{:S(2)}, u32[]{:S(2)}) async-start(bf16[16,256,512]{2,1,0:T(8,128)(2,1)} %maximum_bitcast_fusion), calls=%async_computation | async-start | bytes 8388608 | tf_op jit(solution)/shard_map/all_to_all | solution.py:144
  76.6 45.8 %all-to-all-start.1 = ((bf16[16,256,256]{2,1,0:T(8,128)(2,1)}), bf16[16,256,256]{2,1,0:T(8,128)(2,1)S(1)}, u32[]{:S(2)}, u32[]{:S(2)}) async-start(bf16[16,256,256]{2,1,0:T(8,128)(2,1)} %maximum_bitcast_fusion.1), calls=%async_computation.1 | async-start | bytes 4194304 | tf_op jit(solution)/shard_map/all_to_all | solution.py:144
  83.6 36.4 %collective-permute-start = (bf16[1024,256]{1,0:T(8,128)(2,1)S(1)}, bf16[1024,256]{1,0:T(8,128)(2,1)S(1)}, u32[]{:S(2)}, u32[]{:S(2)}) collective-permute-start(bf16[1024,256]{1,0:T(8,128)(2,1)S(1)} %slice.100), channel_id=1, source_target_pairs={{0,16},{16,32},{32,48},{48,64},{64,80},{80,96},{96,112},{1,17},{17... | collective-permute-start | bytes 1572872 | tf_op jit(solution)/shard_map/ppermute | solution.py:21
  91.0 29.0 %copy-start.5 = (bf16[4096,128]{1,0:T(8,128)(2,1)S(1)}, bf16[4096,128]{1,0:T(8,128)(2,1)}, u32[]{:S(2)}) copy-start(bf16[4096,128]{1,0:T(8,128)(2,1)} %get-tuple-element.28.refs_3_) | copy-start | bytes 3145732
  116.4 4.8 %copy-start.4 = (bf16[4096,128]{1,0:T(8,128)(2,1)S(1)}, bf16[4096,128]{1,0:T(8,128)(2,1)}, u32[]{:S(2)}) copy-start(bf16[4096,128]{1,0:T(8,128)(2,1)} %get-tuple-element.29.refs_2_) | copy-start | bytes 3145732
  122.4 2.0 copy-start.2
  143.6 54.5 %all-to-all-start.2 = ((bf16[16,256,256]{2,1,0:T(8,128)(2,1)}), bf16[16,256,256]{2,1,0:T(8,128)(2,1)S(1)}, u32[]{:S(2)}, u32[]{:S(2)}) async-start(bf16[16,256,256]{2,1,0:T(8,128)(2,1)} %bitcast.49), calls=%async_computation.2 | async-start | bytes 4194304 | tf_op jit(solution)/shard_map/all_to_all | solution.py:151
  153.1 34.7 %collective-permute-start.1 = (bf16[1024,256]{1,0:T(8,128)(2,1)S(1)}, bf16[1024,256]{1,0:T(8,128)(2,1)S(1)}, u32[]{:S(2)}, u32[]{:S(2)}) collective-permute-start(bf16[1024,256]{1,0:T(8,128)(2,1)S(1)} %pad_maximum_fusion.2), channel_id=1, source_target_pairs={{16,0},{32,16},{48,32},{64,48},{80,64},{96,80},{112,96},{17,1},{33... | collective-permute-start | bytes 1572872 | tf_op jit(solution)/shard_map/ppermute | solution.py:21
  185.4 3.8 %copy-start.3 = (bf16[4096,256]{1,0:T(8,128)(2,1)S(1)}, bf16[4096,256]{1,0:T(8,128)(2,1)}, u32[]{:S(2)}) copy-start(bf16[4096,256]{1,0:T(8,128)(2,1)} %get-tuple-element.21) | copy-start | bytes 6291460
  198.1 68.5 %all-to-all-start.3 = ((bf16[16,256,512]{2,1,0:T(8,128)(2,1)}), bf16[16,256,512]{2,1,0:T(8,128)(2,1)}, u32[]{:S(2)}, u32[]{:S(2)}) async-start(bf16[16,256,512]{2,1,0:T(8,128)(2,1)} %bitcast.45), calls=%async_computation.3 | async-start | bytes 8388608 | tf_op jit(solution)/shard_map/all_to_all | solution.py:151
  272.2 1.6 copy-start.6
  273.8 1.9 copy-start.1

commit v5 on v4

--- a/solution.py
+++ b/solution.py
@@ -21,17 +21,29 @@
     return lax.ppermute(block, axis, route)
 
 
-def attend_kernel(first_ref, *refs, heads, block_offset, key_shift, carry):
-    q_refs = refs[0 : 2 * heads : 2]
-    g_refs = refs[1 : 2 * heads : 2]
-    k_ref, v_ref = refs[2 * heads : 2 * heads + 2]
-    rest = refs[2 * heads + 2 :]
-    if carry:
-        rest = rest[heads:]
-        dk_in_ref, dv_in_ref = rest[:2]
-        rest = rest[2:]
-    od_refs = rest[:heads]
-    dk_ref, dv_ref = rest[heads:]
+def attend_kernel(first_ref, *refs, heads, block_offset, early, carry_od, carry_acc):
+    pos = 0
+    q_refs, g_refs = [], []
+    for _ in range(heads):
+        q_refs.append(refs[pos])
+        g_refs.append(refs[pos + 1])
+        pos += 2
+    if early:
+        kt_ref, vt_ref, kg_ref, vg_ref = refs[pos : pos + 4]
+        pos += 4
+    else:
+        k_ref, v_ref = refs[pos : pos + 2]
+        pos += 2
+    pos += sum(carry_od)
+    if carry_acc:
+        dk_in_ref, dv_in_ref = refs[pos : pos + 2]
+        pos += 2
+    od_refs = refs[pos : pos + heads]
+    pos += heads
+    dk_ref, dv_ref, bias_ref = refs[pos : pos + 3]
+    pos += 3
+    if early:
+        kx_ref, vx_ref = refs[pos : pos + 2]
     step = pl.program_id(0)
     block = step + block_offset
     rows = q_refs[0].shape[0]
@@ -40,22 +52,35 @@
 
     @pl.when(step == 0)
     def _():
-        if carry:
+        if carry_acc:
             dk_ref[...] = dk_in_ref[...]
             dv_ref[...] = dv_in_ref[...]
         else:
             dk_ref[...] = jnp.zeros_like(dk_ref)
             dv_ref[...] = jnp.zeros_like(dv_ref)
+        row_id = lax.broadcasted_iota(jnp.int32, (rows, span), 0)
+        col_id = lax.broadcasted_iota(jnp.int32, (rows, span), 1)
+        distance = row_id + WIN - col_id
+        band = (distance >= 0) & (distance < WIN)
+        bias_ref[...] = jnp.where(band, 0.0, -jnp.inf).astype(jnp.float32)
+        if early:
+            kx_ref[:WIN, :] = kt_ref[...]
+            kx_ref[WIN:, :] = kg_ref[...]
+            vx_ref[:WIN, :] = vt_ref[...]
+            vx_ref[WIN:, :] = vg_ref[...]
 
     start = pl.multiple_of(block * rows, rows)
-    key_start = pl.multiple_of(block * rows - key_shift, rows)
-    k_win = k_ref[pl.ds(key_start, span), :]
-    v_win = v_ref[pl.ds(key_start, span), :]
-    row_id = lax.broadcasted_iota(jnp.int32, (rows, span), 0)
-    col_id = lax.broadcasted_iota(jnp.int32, (rows, span), 1)
-    distance = row_id + WIN - col_id
-    key_pos = first_ref[0] - WIN + start + col_id
-    allowed = (distance >= 0) & (distance < WIN) & (key_pos >= 0)
+    if early:
+        k_win = kx_ref[pl.ds(start, span), :]
+        v_win = vx_ref[pl.ds(start, span), :]
+        col_id = lax.broadcasted_iota(jnp.int32, (rows, span), 1)
+        key_pos = first_ref[0] - WIN + start + col_id
+        bias = jnp.where(key_pos >= 0, bias_ref[...], -jnp.inf)
+    else:
+        key_start = pl.multiple_of(start - WIN, rows)
+        k_win = k_ref[pl.ds(key_start, span), :]
+        v_win = v_ref[pl.ds(key_start, span), :]
+        bias = bias_ref[...]
     nt = (((1,), (1,)), ((), ()))
     tn = (((0,), (0,)), ((), ()))
     dk_acc = None
@@ -64,7 +89,7 @@
         q = q_ref[...]
         g = g_ref[...]
         scores = lax.dot_general(q, k_win, nt, preferred_element_type=jnp.float32) * scale
-        scores = jnp.where(allowed, scores, -jnp.inf)
+        scores = scores + bias
         largest = jnp.max(scores, axis=-1, keepdims=True)
         unnormed = jnp.exp(scores - largest)
         probs = unnormed * (1.0 / jnp.sum(unnormed, axis=-1, keepdims=True))
@@ -85,14 +110,15 @@
     dv_ref[pl.ds(start, span), :] += dv_acc
 
 
-def attend(sources, keys, values, first_query, blocks, key_shift, carried=None):
+def attend(sources, first_part, tail, first_query, blocks, carried_od, carried_acc):
     heads = len(sources)
-    query_count = sources[0][0].shape[0]
+    query_count = first_part.shape[0]
     ext_rows = WIN + query_count
     rows = BLK
+    span = WIN + rows
     block_offset, block_count = blocks
+    early = tail is not None
     first = jnp.reshape(first_query, (1,)).astype(jnp.int32)
-    key_spec = pl.BlockSpec(keys.shape, lambda b, f: (0, 0))
     whole = pl.BlockSpec((ext_rows, HD), lambda b, f: (0, 0))
     in_specs = []
     operands = [first]
@@ -102,27 +128,51 @@
             pl.BlockSpec((rows, HD), lambda b, f, c=g_col: (b + block_offset, c)),
         ]
         operands += [source, source]
-    in_specs += [key_spec, key_spec]
-    operands += [keys, values]
+    if early:
+        piece = (WIN, HD)
+        in_specs += [
+            pl.BlockSpec(piece, lambda b, f: (0, 0)),
+            pl.BlockSpec(piece, lambda b, f: (0, 1)),
+            pl.BlockSpec(piece, lambda b, f: (0, 0)),
+            pl.BlockSpec(piece, lambda b, f: (0, 1)),
+        ]
+        operands += [tail, tail, first_part, first_part]
+    else:
+        in_specs += [
+            pl.BlockSpec((query_count, HD), lambda b, f: (0, 0)),
+            pl.BlockSpec((query_count, HD), lambda b, f: (0, 1)),
+        ]
+        operands += [first_part, first_part]
     aliases = {}
-    if carried is not None:
-        base = len(operands)
-        in_specs += [pl.BlockSpec(memory_space=pl.ANY)] * heads + [whole, whole]
-        operands += list(carried)
-        aliases = {base + i: i for i in range(heads + 2)}
+    carry_od = tuple(od is not None for od in carried_od)
+    for i, od in enumerate(carried_od):
+        if od is not None:
+            aliases[len(operands)] = i
+            in_specs.append(pl.BlockSpec(memory_space=pl.ANY))
+            operands.append(od)
+    if carried_acc is not None:
+        aliases[len(operands)] = heads
+        aliases[len(operands) + 1] = heads + 1
+        in_specs += [whole, whole]
+        operands += list(carried_acc)
+    scratch = [pltpu.VMEM((rows, span), jnp.float32)]
+    if early:
+        scratch += [pltpu.VMEM((2 * WIN, HD), jnp.bfloat16)] * 2
     grid_spec = pltpu.PrefetchScalarGridSpec(
         num_scalar_prefetch=1,
         grid=(block_count,),
         in_specs=in_specs,
         out_specs=[pl.BlockSpec((rows, 2 * HD), lambda b, f: (b + block_offset, 0))] * heads
         + [whole, whole],
+        scratch_shapes=scratch,
     )
     kernel = functools.partial(
         attend_kernel,
         heads=heads,
         block_offset=block_offset,
-        key_shift=key_shift,
-        carry=carried is not None,
+        early=early,
+        carry_od=carry_od,
+        carry_acc=carried_acc is not None,
     )
     return pl.pallas_call(
         kernel,
@@ -168,43 +218,40 @@
     block_total = group_rows // BLK
     lead = WIN // BLK
     first_query = lax.axis_index("ctx") * group_rows
-    group_keys = first_part[:, :HD]
-    group_values = first_part[:, HD : 2 * HD]
     tail = shifted(first_part[group_rows - WIN :, : 2 * HD], "ctx", 1)
     late = (lead, block_total - lead)
     early = (0, lead)
     head0 = (first_part, 2, 3)
     head1 = (second_part, 0, 1)
-    carried = attend([head0], group_keys, group_values, first_query, late, WIN)
-    keys_ext = jnp.concatenate([tail[:, :HD], group_keys], axis=0)
-    values_ext = jnp.concatenate([tail[:, HD:], group_values], axis=0)
+    first_out, key_acc, value_acc = attend(
+        [head0], first_part, None, first_query, late, (None,), None
+    )
     first_out, second_out, key_acc, value_acc = attend(
-        [head0, head1], keys_ext, values_ext, first_query, early, 0,
-        (carried[0], jnp.zeros_like(carried[0]), carried[1], carried[2]),
+        [head0, head1], first_part, tail, first_query, early, (first_out, None),
+        (key_acc, value_acc),
     )
     back = shifted(
         jnp.concatenate([key_acc[:WIN], value_acc[:WIN]], axis=1).astype(jnp.bfloat16), "ctx", -1
     ).astype(jnp.float32)
     second_out, key_total, value_total = attend(
-        [head1], keys_ext, values_ext, first_query, late, 0, (second_out, key_acc, value_acc)
-    )
+        [head1], first_part, None, first_query, late, (second_out,), (key_acc, value_acc)
+    )
+    first_back = exchange_out(first_out)
+    second_back = exchange_out(second_out)
     key_grad = jnp.concatenate(
         [key_total[WIN:group_rows], key_total[group_rows:] + back[:, :HD]], axis=0
     ).astype(jnp.bfloat16)
     value_grad = jnp.concatenate(
         [value_total[WIN:group_rows], value_total[group_rows:] + back[:, HD:]], axis=0
     ).astype(jnp.bfloat16)
-    first_back = exchange_out(first_out)
-    second_back = exchange_out(jnp.concatenate([second_out, key_grad, value_grad], axis=1))
+    grads_back = exchange_out(jnp.concatenate([key_grad, value_grad], axis=1))
     attended = jnp.concatenate([first_back[:, :, :HD], second_back[:, :, :HD]], axis=2)
-    grad_queries = jnp.concatenate(
-        [first_back[:, :, HD:], second_back[:, :, HD : 2 * HD]], axis=2
-    )
+    grad_queries = jnp.concatenate([first_back[:, :, HD:], second_back[:, :, HD:]], axis=2)
     return (
         attended.reshape(token_count, QH * HD),
         grad_queries.reshape(token_count, QH * HD),
-        second_back[:, :, 2 * HD : 3 * HD].reshape(token_count, KVH * HD),
-        second_back[:, :, 3 * HD :].reshape(token_count, KVH * HD),
+        grads_back[:, :, :HD].reshape(token_count, KVH * HD),
+        grads_back[:, :, HD:].reshape(token_count, KVH * HD),
     )
 
 

time: 278 us -> 265 us (0.953)
  other arithmetic: 17.2 us -> 6.51 us
  starting transfers between devices: 34.3 us -> 40.4 us
  local copies, waits for them, and re-layouts: 28.2 us -> 22.7 us
    all_to_all x2 -> x3, waiting for transfers between devices: 59.8 us -> 23.2 us  [exchange_out(): lax.all_to_all(split, 'head', split_axis=0, concat_axis=0, tiled=True)]
    ppermute x2, waiting for transfers between devices: 4.3 us -> 39.6 us  [shifted(): return lax.ppermute(block, axis, route)]
    concatenate x3, other arithmetic: 11.3 us -> 1.75 us  [the longest x1 1.61 us: body(): grads_back = exchange_out(jnp.concatenate([key_grad, value_grad], axis=1))]
    all_to_all x2 -> x3, starting transfers between devices: 14.5 us -> 20.6 us  [exchange_out(): lax.all_to_all(split, 'head', split_axis=0, concat_axis=0, tiled=True)]
    unnamed x25 -> x27, local copies, waits for them, and re-layouts: 8.74 us -> 10.1 us
  transfers between devices with their start and end apart: 6 -> 7, of which waited for: 4 -> 4; matrix products, arithmetic and copies ran while one was open for 9% -> 5% of each run, Pallas kernels for 19% -> 20%
where the time goes in v5:
time: 265 us; the launch traced here: 264 us
  waiting for transfers between devices  122 us (46%)
  Pallas kernels  71.3 us (27%)
  starting transfers between devices  40.4 us (15%)
  local copies, waits for them, and re-layouts  22.7 us (9%)
  other arithmetic  6.51 us (2%)
    pallas_call x3, Pallas kernels, attend(): pl.pallas_call(kernel, grid_spec=grid_spec, out_shape=[jax.ShapeDtypeStru...  71.3 us
    all_to_all x2, waiting for transfers between devices, exchange_in(): lax.all_to_all(stacked, 'head', split_axis=0, concat_axis=0, tiled=True)  59.2 us
    ppermute x2, waiting for transfers between devices, shifted(): return lax.ppermute(block, axis, route)  39.6 us
    all_to_all x3, waiting for transfers between devices, exchange_out(): lax.all_to_all(split, 'head', split_axis=0, concat_axis=0, tiled=True)  23.2 us
    all_to_all x3, starting transfers between devices, exchange_out(): lax.all_to_all(split, 'head', split_axis=0, concat_axis=0, tiled=True)  20.6 us
    all_to_all x2, starting transfers between devices, exchange_in(): lax.all_to_all(stacked, 'head', split_axis=0, concat_axis=0, tiled=True)  11.9 us
    unnamed x27, local copies, waits for them, and re-layouts  10.1 us
    ppermute x2, starting transfers between devices, shifted(): return lax.ppermute(block, axis, route)  8 us
  transfers between devices with their start and end apart: 7, of which 4 were waited for; matrix products, arithmetic and copies ran while one was open for 5% of the time, Pallas kernels for 20%

profile of v5, /device:TPU:121, one launch (start us, length us, event | category | flops | bytes accessed | tf_op | source)
XLA Modules:
  0.0 263.8 jit_solution(6418608374719894397)
XLA Ops:
  0.6 2.3 copy.34
  3.6 1.3 copy-done.8
  4.9 0.6 copy.35
  6.3 0.9 copy-done.9
  7.7 2.3 maximum_bitcast_fusion
  10.0 5.9 %all-to-all-start = ((bf16[16,256,512]{2,1,0:T(8,128)(2,1)}), bf16[16,256,512]{2,1,0:T(8,128)(2,1)}, u32[]{:S(2)}, u32[]{:S(2)}) async-start(bf16[16,256,512]{2,1,0:T(8,128)(2,1)} %maximum_bitcast_fusion), calls=%async_computation | async-start | bytes 8388608 | tf_op jit(solution)/shard_map/all_to_all | solution.py:194
  16.5 1.6 maximum_bitcast_fusion.1
  18.1 59.2 %all-to-all-done = bf16[16,256,512]{2,1,0:T(8,128)(2,1)} async-done(((bf16[16,256,512]{2,1,0:T(8,128)(2,1)}), bf16[16,256,512]{2,1,0:T(8,128)(2,1)}, u32[]{:S(2)}, u32[]{:S(2)}) %all-to-all-start) | async-done | bytes 4194336 | tf_op jit(solution)/shard_map/all_to_all | solution.py:194
  77.3 5.9 %all-to-all-start.1 = ((bf16[16,256,256]{2,1,0:T(8,128)(2,1)}), bf16[16,256,256]{2,1,0:T(8,128)(2,1)S(1)}, u32[]{:S(2)}, u32[]{:S(2)}) async-start(bf16[16,256,256]{2,1,0:T(8,128)(2,1)} %maximum_bitcast_fusion.1), calls=%async_computation.1 | async-start | bytes 4194304 | tf_op jit(solution)/shard_map/all_to_all | solution.py:194
  83.2 1.1 slice.84
  84.3 4.4 %collective-permute-start = (bf16[1024,256]{1,0:T(8,128)(2,1)S(1)}, bf16[1024,256]{1,0:T(8,128)(2,1)S(1)}, u32[]{:S(2)}, u32[]{:S(2)}) collective-permute-start(bf16[1024,256]{1,0:T(8,128)(2,1)S(1)} %slice.84), channel_id=1, source_target_pairs={{0,16},{16,32},{32,48},{48,64},{64,80},{80,96},{96,112},{1,17},{17... | collective-permute-start | bytes 1572872 | tf_op jit(solution)/shard_map/ppermute | solution.py:21
  88.7 25.4 %shard_map.75 = (bf16[4096,256]{1,0:T(8,128)(2,1)}, f32[5120,128]{1,0:T(8,128)}, f32[5120,128]{1,0:T(8,128)}) custom-call(s32[1]{0:T(128)} %bitcast.first_ref, bf16[4096,512]{1,0:T(8,128)(2,1)} %bitcast.2.refs_0_.refs_1_.refs_2_.refs_3_.refs_6_.refs_7_, bf16[4096,512]{1,0:T(8,128)(2,1)} %bitcast.2.refs_0_.refs_1_.refs_2_.refs_3_.refs_6_.refs_7_, ...), custom_call_target="tpu_custom_call" | custom-call | tf_op jit(solution)/shard_map/pallas_call | solution.py:177
  114.1 6.6 %collective-permute-done.refs_4_.refs_5_ = bf16[1024,256]{1,0:T(8,128)(2,1)S(1)} collective-permute-done((bf16[1024,256]{1,0:T(8,128)(2,1)S(1)}, bf16[1024,256]{1,0:T(8,128)(2,1)S(1)}, u32[]{:S(2)}, u32[]{:S(2)}) %collective-permute-start) | collective-permute-done | bytes 524320 | tf_op jit(solution)/shard_map/ppermute | solution.py:21
  120.7 0.8 copy-done.7
  121.5 18.9 %shard_map.76 = (bf16[4096,256]{1,0:T(8,128)(2,1)}, bf16[4096,256]{1,0:T(8,128)(2,1)}, f32[5120,128]{1,0:T(8,128)}, f32[5120,128]{1,0:T(8,128)}) custom-call(s32[1]{0:T(128)} %bitcast.first_ref, bf16[4096,512]{1,0:T(8,128)(2,1)} %bitcast.2.refs_0_.refs_1_.refs_2_.refs_3_.refs_6_.refs_7_, ...), custom_call_target="tpu_custom_call", output_to_operand_aliasing={{0}: (9, {}), {2}: (10, {}), {3}: (11, {})} | custom-call | tf_op jit(solution)/shard_map/pallas_call | solution.py:177
  140.4 7.2 %all-to-all-start.2 = ((bf16[16,256,256]{2,1,0:T(8,128)(2,1)}), bf16[16,256,256]{2,1,0:T(8,128)(2,1)S(1)}, u32[]{:S(2)}, u32[]{:S(2)}) async-start(bf16[16,256,256]{2,1,0:T(8,128)(2,1)} %bitcast.52), calls=%async_computation.2 | async-start | bytes 4194304 | tf_op jit(solution)/shard_map/all_to_all | solution.py:201
  147.7 1.1 slice.114
  148.7 1.1 slice.113
  149.8 27.0 %shard_map.77 = (bf16[4096,256]{1,0:T(8,128)(2,1)}, f32[5120,128]{1,0:T(8,128)}, f32[5120,128]{1,0:T(8,128)}) custom-call(s32[1]{0:T(128)} %bitcast.first_ref, bf16[4096,256]{1,0:T(8,128)(2,1)} %bitcast.46, bf16[4096,256]{1,0:T(8,128)(2,1)} %bitcast.47, ...), custom_call_target="tpu_custom_call", output_to_operand_aliasing={{0}: (5, {}), {1}: (6, {}), {2}: (7, {})} | custom-call | tf_op jit(solution)/shard_map/pallas_call | solution.py:177
  176.8 1.3 copy-done.5
  178.1 6.0 %all-to-all-start.3 = ((bf16[16,256,256]{2,1,0:T(8,128)(2,1)}), bf16[16,256,256]{2,1,0:T(8,128)(2,1)}, u32[]{:S(2)}, u32[]{:S(2)}) async-start(bf16[16,256,256]{2,1,0:T(8,128)(2,1)} %bitcast.51), calls=%async_computation.3 | async-start | bytes 4194304 | tf_op jit(solution)/shard_map/all_to_all | solution.py:201
  184.2 3.6 %collective-permute-start.1 = (bf16[1024,256]{1,0:T(8,128)(2,1)S(1)}, bf16[1024,256]{1,0:T(8,128)(2,1)S(1)}, u32[]{:S(2)}, u32[]{:S(2)}) collective-permute-start(bf16[1024,256]{1,0:T(8,128)(2,1)S(1)} %pad_maximum_fusion.3), channel_id=1, source_target_pairs={{16,0},{32,16},{48,32},{64,48},{80,64},{96,80},{112,96},{17,1},{33... | collective-permute-start | bytes 1572872 | tf_op jit(solution)/shard_map/ppermute | solution.py:21
  188.0 33.0 %collective-permute-done.1 = bf16[1024,256]{1,0:T(8,128)(2,1)S(1)} collective-permute-done((bf16[1024,256]{1,0:T(8,128)(2,1)S(1)}, bf16[1024,256]{1,0:T(8,128)(2,1)S(1)}, u32[]{:S(2)}, u32[]{:S(2)}) %collective-permute-start.1) | collective-permute-done | bytes 524320 | tf_op jit(solution)/shard_map/ppermute | solution.py:21
  221.4 1.6 pad_maximum_fusion
  223.0 7.4 %all-to-all-start.4 = ((bf16[16,256,256]{2,1,0:T(8,128)(2,1)}), bf16[16,256,256]{2,1,0:T(8,128)(2,1)}, u32[]{:S(2)}, u32[]{:S(2)}) async-start(bf16[16,256,256]{2,1,0:T(8,128)(2,1)} %pad_maximum_fusion), calls=%async_computation.4 | async-start | bytes 4194304 | tf_op jit(solution)/shard_map/all_to_all | solution.py:201
  231.0 1.7 fusion.3
  232.9 1.6 copy.31
  234.8 1.6 copy.30
  236.4 23.1 %all-to-all-done.4 = bf16[16,256,256]{2,1,0:T(8,128)(2,1)} async-done(((bf16[16,256,256]{2,1,0:T(8,128)(2,1)}), bf16[16,256,256]{2,1,0:T(8,128)(2,1)}, u32[]{:S(2)}, u32[]{:S(2)}) %all-to-all-start.4) | async-done | bytes 2097184 | tf_op jit(solution)/shard_map/all_to_all | solution.py:201
  259.6 1.7 slice_bitcast_fusion
  261.3 1.3 copy.40
  262.5 1.3 copy.41
  (36 shorter events, 4.1 us)
Async XLA Ops:
  0.6 5.6 %copy-start = (bf16[256,2048]{1,0:T(8,128)(2,1)S(1)}, bf16[256,2048]{1,0:T(8,128)(2,1)}, u32[]{:S(2)}) copy-start(bf16[256,2048]{1,0:T(8,128)(2,1)} %param.5) | copy-start | bytes 3145732
  3.3 1.6 copy-start.8
  6.0 1.2 copy-start.9
  10.0 67.3 %all-to-all-start = ((bf16[16,256,512]{2,1,0:T(8,128)(2,1)}), bf16[16,256,512]{2,1,0:T(8,128)(2,1)}, u32[]{:S(2)}, u32[]{:S(2)}) async-start(bf16[16,256,512]{2,1,0:T(8,128)(2,1)} %maximum_bitcast_fusion), calls=%async_computation | async-start | bytes 8388608 | tf_op jit(solution)/shard_map/all_to_all | solution.py:194
  77.3 36.8 %all-to-all-start.1 = ((bf16[16,256,256]{2,1,0:T(8,128)(2,1)}), bf16[16,256,256]{2,1,0:T(8,128)(2,1)S(1)}, u32[]{:S(2)}, u32[]{:S(2)}) async-start(bf16[16,256,256]{2,1,0:T(8,128)(2,1)} %maximum_bitcast_fusion.1), calls=%async_computation.1 | async-start | bytes 4194304 | tf_op jit(solution)/shard_map/all_to_all | solution.py:194
  84.3 36.4 %collective-permute-start = (bf16[1024,256]{1,0:T(8,128)(2,1)S(1)}, bf16[1024,256]{1,0:T(8,128)(2,1)S(1)}, u32[]{:S(2)}, u32[]{:S(2)}) collective-permute-start(bf16[1024,256]{1,0:T(8,128)(2,1)S(1)} %slice.84), channel_id=1, source_target_pairs={{0,16},{16,32},{32,48},{48,64},{64,80},{80,96},{96,112},{1,17},{17... | collective-permute-start | bytes 1572872 | tf_op jit(solution)/shard_map/ppermute | solution.py:21
  114.1 6.6 %copy-start.2 = (bf16[16,256,256]{2,1,0:T(8,128)(2,1)}, bf16[16,256,256]{2,1,0:T(8,128)(2,1)S(1)}, u32[]{:S(2)}) copy-start(bf16[16,256,256]{2,1,0:T(8,128)(2,1)S(1)} %all-to-all-done.1) | copy-start | bytes 6291460
  120.7 0.8 copy-start.7
  140.4 36.4 %all-to-all-start.2 = ((bf16[16,256,256]{2,1,0:T(8,128)(2,1)}), bf16[16,256,256]{2,1,0:T(8,128)(2,1)S(1)}, u32[]{:S(2)}, u32[]{:S(2)}) async-start(bf16[16,256,256]{2,1,0:T(8,128)(2,1)} %bitcast.52), calls=%async_computation.2 | async-start | bytes 4194304 | tf_op jit(solution)/shard_map/all_to_all | solution.py:201
  176.8 1.3 copy-start.5
  178.1 9.7 %copy-start.4 = (f32[5120,128]{1,0:T(8,128)S(1)}, f32[5120,128]{1,0:T(8,128)}, u32[]{:S(2)}) copy-start(f32[5120,128]{1,0:T(8,128)} %get-tuple-element.23) | copy-start | bytes 7864324
  178.1 44.9 %all-to-all-start.3 = ((bf16[16,256,256]{2,1,0:T(8,128)(2,1)}), bf16[16,256,256]{2,1,0:T(8,128)(2,1)}, u32[]{:S(2)}, u32[]{:S(2)}) async-start(bf16[16,256,256]{2,1,0:T(8,128)(2,1)} %bitcast.51), calls=%async_computation.3 | async-start | bytes 4194304 | tf_op jit(solution)/shard_map/all_to_all | solution.py:201
  184.1 3.8 %copy-start.3 = (f32[5120,128]{1,0:T(8,128)S(1)}, f32[5120,128]{1,0:T(8,128)}, u32[]{:S(2)}) copy-start(f32[5120,128]{1,0:T(8,128)} %get-tuple-element.22) | copy-start | bytes 7864324
  184.2 36.9 %collective-permute-start.1 = (bf16[1024,256]{1,0:T(8,128)(2,1)S(1)}, bf16[1024,256]{1,0:T(8,128)(2,1)S(1)}, u32[]{:S(2)}, u32[]{:S(2)}) collective-permute-start(bf16[1024,256]{1,0:T(8,128)(2,1)S(1)} %pad_maximum_fusion.3), channel_id=1, source_target_pairs={{16,0},{32,16},{48,32},{64,48},{80,64},{96,80},{112,96},{17,1},{33... | collective-permute-start | bytes 1572872 | tf_op jit(solution)/shard_map/ppermute | solution.py:21
  223.0 7.4 %copy-start.6 = (bf16[16,256,256]{2,1,0:T(8,128)(2,1)S(1)}, bf16[16,256,256]{2,1,0:T(8,128)(2,1)}, u32[]{:S(2)}) copy-start(bf16[16,256,256]{2,1,0:T(8,128)(2,1)} %copy-done.5) | copy-start | bytes 6291460
  223.0 36.5 %all-to-all-start.4 = ((bf16[16,256,256]{2,1,0:T(8,128)(2,1)}), bf16[16,256,256]{2,1,0:T(8,128)(2,1)}, u32[]{:S(2)}, u32[]{:S(2)}) async-start(bf16[16,256,256]{2,1,0:T(8,128)(2,1)} %pad_maximum_fusion), calls=%async_computation.4 | async-start | bytes 4194304 | tf_op jit(solution)/shard_map/all_to_all | solution.py:201
  261.2 2.5 copy-start.1
